TPU v7x, 256 devices: a whole 4x4x8 slice. The times are simulated.
256 devices in a mesh: req: 64 (over y_lo, z, x), tp: 4 (over y_hi, core).
Axes of the slice: x: 4, y: 4 (y_hi: 2, y_lo: 2; y = y_hi * 2 + y_lo), z: 8, core: 2. Of those that a mesh axis runs over, the one named last changes fastest.
Arguments:
- query_heads: bfloat16 [61440, 4096], P('req', 'tp'), parts along dimension 0, may hold values from -140 to 140
- normed_key_heads: bfloat16 [61440, 512], P('req', 'tp'), parts along dimension 0, may hold values from -7 to 7
- value_rows_per_head: bfloat16 [61440, 512], P('req', 'tp'), parts along dimension 0, may hold values from -6 to 6
- residual_in: bfloat16 [61440, 2048], P(('req', 'tp')), parts along dimension 0, may hold values from -6 to 6
- out_weight: bfloat16 [4096, 2048], P('tp'), may hold values from -0.09375 to 0.09375
- norm_gain: float32 [2048], replicated, may hold values from 0.3 to 3
- gate_up: bfloat16 [2, 2, 2048, 768], P(None, None, None, 'tp'), may hold values from -0.125 to 0.125
- down_weight: bfloat16 [2, 768, 2048], P(None, 'tp'), may hold values from -0.21875 to 0.21875
- segment_ids: int32 [61440], P('req'), parts along dimension 0, may hold values from 0 to 5, never falling along the last dimension, each value on 1 to 480 neighbouring positions
- expert_ids: int32 [61440, 8], P('req'), parts along dimension 0, may hold values from 0 to 127, all different within a row; in each aligned block of 960 rows (0 to 959, 960 to 1919, ...) at most 75 rows name the same one
- gate_weights: float32 [61440, 8], P('req'), parts along dimension 0, may hold values from 0.05 to 0.8
Outputs:
- layer_out: bfloat16 [61440, 2048], P(('req', 'tp')), parts along dimension 0
There are 64 independent parts, one for each index of `req`. A program takes and returns all parts, laid end to end along the dimension named above; an argument that names none is the same for every part. Nothing has to cross between parts.
Inputs may be any that keep to these rules, and one draw needn't show every extreme that they name: `segment_ids`: segment ids never fall along the tokens; each prompt has 1 to 480 tokens and one has exactly 480. `expert_ids`: the 8 experts of a token are distinct; no expert is chosen by more than 75 tokens of a request group, a bound that some block reaches.
All inputs are finite; a program needn't handle non-finite values.
Results may differ from a plain program's by a relative error of at most 0.0053.
Values may be sent and summed in bfloat16 or wider, within the bound.
No kernel may reach another device: no remote copies, remote signals or barrier semaphores. Data moves between devices by JAX's collectives and lax.ppermute only.
A program may use at most 128 MiB of HBM per device.

v0:
```python
import math

import jax
import jax.numpy as jnp
from jax import lax
from jax.sharding import PartitionSpec as P

QUERY_HEADS = 32
KEY_VALUE_HEADS = 4
HEAD_WIDTH = 128
EXPERTS = 128


def positions_of(segment_ids):
    earlier = (segment_ids[None, :] < segment_ids[:, None]).astype(jnp.int32)
    return jnp.arange(segment_ids.shape[0], dtype=jnp.int32) - jnp.sum(earlier, axis=1)


def rotary_tables(vectors, token_positions):
    half_dim = vectors.shape[-1] // 2
    frequency = 1000000.0 ** (-jnp.arange(half_dim, dtype=jnp.float32) / half_dim)
    angles = token_positions.astype(jnp.float32)[:, None] * frequency[None, :]
    cosine = jnp.cos(angles)[:, None, :]
    sine = jnp.sin(angles)[:, None, :]
    first = vectors[..., :half_dim]
    second = vectors[..., half_dim:]
    return jnp.concatenate(
        [first * cosine - second * sine, second * cosine + first * sine], axis=-1
    )


def rms_norm(hidden, gain):
    widened = hidden.astype(jnp.float32)
    factor = lax.rsqrt(jnp.mean(widened * widened, axis=-1, keepdims=True) + 1e-06)
    return (widened * factor * gain).astype(jnp.bfloat16)


SEG_MOST = 480


def xor_pairs(size, mask):
    return [(index, index ^ mask) for index in range(size)]


def attend_blocks(query_heads, firsts, rows, keys_after_rotary, values, segment_ids, token_positions):
    item_count = segment_ids.shape[0]
    span = min(item_count, rows + SEG_MOST)
    head_count = query_heads.shape[1] // HEAD_WIDTH
    starts = [jnp.clip(first + rows - span, 0, item_count - span) for first in firsts]
    row_index = jnp.stack([first + jnp.arange(rows, dtype=jnp.int32) for first in firsts])
    key_index = jnp.stack([start + jnp.arange(span, dtype=jnp.int32) for start in starts])
    row_segment = jnp.stack([lax.dynamic_slice_in_dim(segment_ids, f, rows) for f in firsts])
    key_segment = jnp.stack([lax.dynamic_slice_in_dim(segment_ids, s, span) for s in starts])
    key_one = jnp.stack([lax.dynamic_slice_in_dim(keys_after_rotary, s, span) for s in starts])
    value_one = jnp.stack([lax.dynamic_slice_in_dim(values, s, span) for s in starts])
    query_rows = jnp.concatenate([lax.dynamic_slice_in_dim(query_heads, f, rows) for f in firsts])
    row_positions = jnp.concatenate(
        [lax.dynamic_slice_in_dim(token_positions, f, rows) for f in firsts]
    )
    queries = rotary_tables(
        query_rows.reshape(len(firsts) * rows, head_count, HEAD_WIDTH).astype(jnp.float32),
        row_positions,
    ).astype(jnp.bfloat16)
    factor = 1.0 / math.sqrt(HEAD_WIDTH)
    stacked = queries.reshape(len(firsts), rows * head_count, HEAD_WIDTH)
    scores = jnp.einsum(
        "nqd,nkd->nqk", stacked, key_one, preferred_element_type=jnp.float32
    ) * factor
    stacked_segment = jnp.repeat(row_segment, head_count, axis=1)
    stacked_index = jnp.repeat(row_index, head_count, axis=1)
    allowed = (stacked_segment[:, :, None] == key_segment[:, None, :]) & (
        key_index[:, None, :] <= stacked_index[:, :, None]
    )
    scores = jnp.where(allowed, scores, -1e30)
    peak = jnp.max(scores, axis=2, keepdims=True)
    weights = jnp.exp(scores - peak)
    weights = (weights / jnp.sum(weights, axis=2, keepdims=True)).astype(jnp.bfloat16)
    attended = jnp.einsum(
        "nqk,nkd->nqd",
        weights,
        value_one,
        preferred_element_type=jnp.float32,
    ).astype(jnp.bfloat16)
    return attended.reshape(len(firsts), rows, head_count, HEAD_WIDTH)


def local(
    query_heads,
    normed_key_heads,
    value_rows_per_head,
    residual_in,
    out_weight,
    norm_gain,
    gate_up,
    down_weight,
    segment_ids,
    expert_ids,
    gate_weights,
):
    tok_rows = residual_in.shape[0]
    group_tokens = expert_ids.shape[0]
    size = lax.axis_size("tp")
    me = lax.axis_index("tp")
    token_positions = positions_of(segment_ids)
    keys_after_rotary = rotary_tables(
        normed_key_heads.reshape(group_tokens, 1, HEAD_WIDTH).astype(jnp.float32), token_positions
    ).astype(jnp.bfloat16)[:, 0]
    values = value_rows_per_head

    def projected_blocks(blocks, queries):
        attended = attend_blocks(
            queries, [block * tok_rows for block in blocks], tok_rows,
            keys_after_rotary, values, segment_ids, token_positions,
        )
        return jnp.einsum(
            "nrhc,hcd->nrd", attended, out_weight.reshape(attended.shape[2], HEAD_WIDTH, -1),
            preferred_element_type=jnp.float32,
        )

    first_pair = projected_blocks([me ^ 3, me ^ 2], query_heads)
    partner_cross = lax.ppermute(first_pair[0].astype(jnp.bfloat16), "tp", xor_pairs(size, 1))
    across = first_pair[1] + partner_cross.astype(jnp.float32)
    across, later_queries = lax.optimization_barrier((across, query_heads))
    from_across = lax.ppermute(across, "tp", xor_pairs(size, 2))
    second_pair = projected_blocks([me ^ 1, me], later_queries)
    partner_own = lax.ppermute(second_pair[0].astype(jnp.bfloat16), "tp", xor_pairs(size, 1))
    projected = (
        second_pair[1]
        + partner_own.astype(jnp.float32)
        + from_across.astype(jnp.float32)
    )
    mixed = (residual_in.astype(jnp.float32) + projected).astype(jnp.bfloat16)
    normed = rms_norm(mixed, norm_gain)

    capacity = min(group_tokens * expert_ids.shape[1] * 5 // (EXPERTS * 4), group_tokens)
    window = gate_up.shape[0]
    slots = jnp.arange(window, dtype=jnp.int32)
    hits = expert_ids[:, :, None] == slots[None, None, :]
    route_all = jnp.sum(jnp.where(hits, gate_weights[:, :, None], 0.0), axis=1)
    chosen = jnp.any(hits, axis=1)
    rank = jnp.cumsum(chosen.astype(jnp.int32), axis=0) - 1
    kk = jnp.arange(-(-capacity // 8) * 8, dtype=jnp.int32)
    select_all = (rank.T[:, None, :] == kk[None, :, None]) & chosen.T[:, None, :]
    route_sel = jnp.sum(jnp.where(select_all, route_all.T[:, None, :], 0.0), axis=-1)
    select_loc = lax.dynamic_slice_in_dim(select_all, me * tok_rows, tok_rows, axis=2)

    picked = jnp.einsum(
        "ekt,td->ekd", select_loc.astype(jnp.bfloat16), normed,
        preferred_element_type=jnp.float32,
    ).astype(jnp.bfloat16)
    picked = picked + lax.ppermute(picked, "tp", xor_pairs(size, 1))
    picked = picked + lax.ppermute(picked, "tp", xor_pairs(size, 2))
    gate = jnp.einsum("ekd,edf->ekf", picked, gate_up[:, 0], preferred_element_type=jnp.float32)
    upward = jnp.einsum("ekd,edf->ekf", picked, gate_up[:, 1], preferred_element_type=jnp.float32)
    active = (jax.nn.silu(gate) * upward).astype(jnp.bfloat16)
    outputs = jnp.einsum("ekf,efd->ekd", active, down_weight, preferred_element_type=jnp.float32)
    scaled = route_sel[:, :, None] * outputs
    scaled = scaled + lax.ppermute(scaled, "tp", xor_pairs(size, 1))
    scaled = scaled + lax.ppermute(
        scaled.astype(jnp.bfloat16), "tp", xor_pairs(size, 2)
    ).astype(jnp.float32)
    experts = jnp.einsum(
        "ekt,ekd->td", select_loc.astype(jnp.float32), scaled,
        precision=lax.Precision.HIGHEST, preferred_element_type=jnp.float32,
    )
    return (mixed.astype(jnp.float32) + experts).astype(jnp.bfloat16)


def solution(mesh):
    placed = (
        P("req", "tp"),
        P("req", "tp"),
        P("req", "tp"),
        P(("req", "tp"), None),
        P("tp", None),
        P(),
        P(None, None, None, "tp"),
        P(None, "tp", None),
        P("req"),
        P("req", None),
        P("req", None),
    )
    return jax.shard_map(
        local, mesh=mesh, in_specs=placed, out_specs=P(("req", "tp"), None), check_vma=False
    )
```

profile of v0, /device:TPU:1, one launch (start us, length us, event | category | flops | bytes accessed | tf_op | source)
XLA Modules:
  0.0 169.4 jit_solution(9944889173166701358)
XLA Ops:
  3.1 1.5 fusion.121
  6.1 1.7 le.35
  11.3 1.7 %eq.60 = s32[2,1920]{1,0:T(2,128)} reshape(s32[2,240,8]{2,1,0:T(8,128)} %broadcast_in_dim.31) | data formatting | bytes 30720 | tf_op jit(solution)/shard_map/eq | solution.py:71
  13.0 1.8 %copy.31 = bf16[960,128]{0,1:T(8,128)(2,1)} copy(bf16[960,128]{1,0:T(8,128)(2,1)} %param.12) | data formatting | bytes 491520 | tf_op args[1]
  15.8 1.8 %fusion.65 = (bf16[960,1,64]{0,2,1:T(8,128)(2,1)S(1)}, bf16[960,1,64]{0,2,1:T(8,128)(2,1)S(1)}) fusion(f32[960,1,128]{0,2,1:T(8,128)S(1)} %bitcast_convert_fusion, f32[64]{0:T(128)} %multiply_power_fusion, f32[960]{0:T(1024)S(1)} %get-tuple-element.44), kind=kLoop, calls=%fused_computation.107 | loop fusion | flops 552960 | bytes 741376 | tf_op jit(solution)/shard_map/convert.13
  17.6 1.4 fusion.73
  19.0 1.7 %copy.33 = bf16[720,1,128]{2,0,1:T(8,128)(2,1)} copy(bf16[720,1,128]{0,2,1:T(8,128)(2,1)} %get-tuple-element.25) | data formatting | bytes 368640 | tf_op jit(solution)/shard_map/dynamic_slice | solution.py:54
  20.7 1.7 %copy.32 = bf16[720,1,128]{2,0,1:T(8,128)(2,1)} copy(bf16[720,1,128]{0,2,1:T(8,128)(2,1)} %get-tuple-element.24) | data formatting | bytes 368640 | tf_op jit(solution)/shard_map/dynamic_slice | solution.py:54
  25.8 2.6 %multiply_cosine_fusion.1 = (f32[480,64]{1,0:T(8,128)}, f32[480,64]{1,0:T(8,128)}, f32[480,64]{1,0:T(8,128)S(1)}, f32[480,64]{1,0:T(8,128)S(1)}) fusion(f32[480]{0:T(512)S(1)} %get-tuple-element.56, f32[64]{0:T(128)S(1)} %copy-done.23, f32[480]{0:T(512)S(1)} %get-tuple-element.55), kind=kLoop, calls=%fused_computation.101 | loop fusion | flops 61440 | bytes 495616 | tf_op jit(solution)/shard_map/cos | solution.py:23
  28.4 2.0 %subtract_convert_fusion.1 = (bf16[480,8,64]{2,1,0:T(8,128)(2,1)}, bf16[480,8,64]{2,1,0:T(8,128)(2,1)}) fusion(f32[480,8,128]{2,1,0:T(8,128)S(1)} %bitcast.105, f32[480,64]{1,0:T(8,128)S(1)} %get-tuple-element.49, f32[480,64]{1,0:T(8,128)S(1)} %get-tuple-element.50), kind=kLoop, calls=%fused_computation.53 | loop fusion | flops 1966080 | bytes 3194880 | tf_op jit(solution)/shard_map/convert.17
  30.4 6.7 %fusion.123 = f32[2,1920]{1,0:T(2,128)} fusion(s32[2,1920]{1,0:T(2,128)} %le.35, s32[2,720]{1,0:T(2,128)} %pad_add_fusion.3, s32[2,720]{1,0:T(2,128)} %pad_add_fusion.2, s32[2,1920]{1,0:T(2,128)} %eq.60, bf16[1,720,128]{2,1,0:T(8,128)(2,1)} %bitcast.115, bf16[1,720,128]{2,1,0:T(8,128)(2,1)} %bitcast.117, bf16[2,1920,64]{2,1,0:T(8,128)(2,1)} %bitcast.113, ...), kind=kOutput, calls=%fused_computation.185 | convolution fusion | flops 729293504 | bytes 1409280 | tf_op jit(solution)/shard_map/sub | solution.py:76
  37.0 9.2 %fusion.39 = bf16[2,240,8,128]{3,2,1,0:T(8,128)(2,1)} fusion(f32[2,1920]{1,0:T(2,128)} %fusion.123, bf16[1,720,128]{2,1,0:T(8,128)(2,1)} %get-tuple-element.28, bf16[1,720,128]{2,1,0:T(8,128)(2,1)} %get-tuple-element.29, s32[2,1920]{1,0:T(2,128)} %le.35, s32[2,720]{1,0:T(2,128)} %pad_add_fusion.3, s32[2,720]{1,0:T(2,128)} %pad_add_fusion.2, ...), kind=kOutput, calls=%fused_computation.62 | convolution fusion | flops 1440526848 | bytes 2760960 | tf_op jit(solution)/shard_map/nqk,nkd->nqd/dot_general | solution.py:78
  46.3 4.2 %convolution_bitcast_fusion.1 = f32[2,240,2048]{2,1,0:T(8,128)S(1)} fusion(bf16[8,128,2048,1]{2,1,0,3:T(8,128)(2,1)} %bitcast.134, bf16[2,240,8,128]{3,2,1,0:T(8,128)(2,1)} %fusion.39), kind=kOutput, calls=%fused_computation.26 | convolution fusion | flops 2013265920 | bytes 9109504 | tf_op jit(solution)/shard_map/nrhc,hcd->nrd/dot_general | solution.py:115
  50.5 1.9 %copy-done.3 = f32[2,240,2048]{2,1,0:T(8,128)} copy-done((f32[2,240,2048]{2,1,0:T(8,128)}, f32[2,240,2048]{2,1,0:T(8,128)S(1)}, u32[]{:S(2)}) %copy-start.3) | copy-done | bytes 3932184
  53.5 3.2 %collective-permute-start = (bf16[240,2048]{1,0:T(8,128)(2,1)}, bf16[240,2048]{1,0:T(8,128)(2,1)}, u32[]{:S(2)}, u32[]{:S(2)}) collective-permute-start(bf16[240,2048]{1,0:T(8,128)(2,1)} %fusion.43), channel_id=1, source_target_pairs={{0,1},{1,0},{2,3},{3,2},{4,5},{5,4},{6,7},{7,6},{8,9},{9,8},{10,11... | collective-permute-start | bytes 2949128 | tf_op jit(solution)/shard_map/ppermute | solution.py:121
  57.6 1.7 le.31
  60.1 1.7 eq.56
  61.8 1.8 %copy.36 = bf16[720,1,128]{2,0,1:T(8,128)(2,1)} copy(bf16[720,1,128]{0,2,1:T(8,128)(2,1)} %get-tuple-element.26) | data formatting | bytes 368640 | tf_op jit(solution)/shard_map/dynamic_slice | solution.py:54
  63.5 1.7 %copy.35 = bf16[720,1,128]{2,0,1:T(8,128)(2,1)} copy(bf16[720,1,128]{0,2,1:T(8,128)(2,1)} %get-tuple-element.23) | data formatting | bytes 368640 | tf_op jit(solution)/shard_map/dynamic_slice | solution.py:54
  66.5 3.4 %fusion.28 = f32[240,2048]{1,0:T(8,128)} fusion(f32[2,240,2048]{2,1,0:T(8,128)} %copy-done.3, bf16[240,2048]{1,0:T(8,128)(2,1)} %collective-permute-done), kind=kLoop, calls=%fused_computation.47 | loop fusion | flops 983040 | bytes 4915200 | tf_op jit(solution)/shard_map/add | solution.py:122
  72.9 6.4 %fusion.124 = f32[2,1920]{1,0:T(2,128)} fusion(s32[2,1920]{1,0:T(2,128)S(1)} %copy-done.16, s32[2,720]{1,0:T(2,128)} %pad_add_fusion.1, s32[2,720]{1,0:T(2,128)} %pad_add_fusion, s32[2,1920]{1,0:T(2,128)} %eq.56, bf16[1,720,128]{2,1,0:T(8,128)(2,1)} %bitcast.119, bf16[1,720,128]{2,1,0:T(8,128)(2,1)} %bitcast.121, bf16[2,1920,64]{2,1,0:T(8,128)(2,1)S(1)} %bitcast.109, ...), kind=kOutput, calls=%fused_computation.186 | convolution fusion | flops 729293504 | bytes 1409280 | tf_op jit(solution)/shard_map/sub | solution.py:76
  79.3 8.9 %fusion.40 = bf16[2,240,8,128]{3,2,1,0:T(8,128)(2,1)} fusion(f32[2,1920]{1,0:T(2,128)} %fusion.124, bf16[1,720,128]{2,1,0:T(8,128)(2,1)} %get-tuple-element.30, bf16[1,720,128]{2,1,0:T(8,128)(2,1)} %get-tuple-element.27, s32[2,1920]{1,0:T(2,128)S(1)} %copy-done.16, s32[2,720]{1,0:T(2,128)} %pad_add_fusion.1, s32[2,720]{1,0:T(2,128)} %pad_add_fusion, ...), kind=kOutput, calls=%fused_computation.63 | convolution fusion | flops 1440526848 | bytes 2760960 | tf_op jit(solution)/shard_map/nqk,nkd->nqd/dot_general | solution.py:78
  88.2 4.2 %convolution_bitcast_fusion = f32[2,240,2048]{2,1,0:T(8,128)S(1)} fusion(bf16[8,128,2048,1]{2,1,0,3:T(8,128)(2,1)} %bitcast.135, bf16[2,240,8,128]{3,2,1,0:T(8,128)(2,1)} %fusion.40), kind=kOutput, calls=%fused_computation.25 | convolution fusion | flops 2013265920 | bytes 9109504 | tf_op jit(solution)/shard_map/nrhc,hcd->nrd/dot_general | solution.py:115
  92.5 1.9 %copy-done.4 = f32[2,240,2048]{2,1,0:T(8,128)} copy-done((f32[2,240,2048]{2,1,0:T(8,128)}, f32[2,240,2048]{2,1,0:T(8,128)S(1)}, u32[]{:S(2)}) %copy-start.4) | copy-done | bytes 3932184
  99.5 16.6 %collective-permute-done.2 = f32[240,2048]{1,0:T(8,128)} collective-permute-done((f32[240,2048]{1,0:T(8,128)}, f32[240,2048]{1,0:T(8,128)}, u32[]{:S(2)}, u32[]{:S(2)}) %collective-permute-start.2) | collective-permute-done | bytes 1966112 | tf_op jit(solution)/shard_map/ppermute | solution.py:124
  116.1 2.7 %fusion.21 = (f32[240]{0:T(256)S(1)}, bf16[240,2048]{1,0:T(8,128)(2,1)S(1)}) fusion(f32[240,2048]{1,0:T(8,128)} %collective-permute-done.2, bf16[240,2048]{1,0:T(8,128)(2,1)S(1)} %collective-permute-done.1, f32[2,240,2048]{2,1,0:T(8,128)} %copy-done.4, bf16[240,2048]{1,0:T(8,128)(2,1)S(1)} %copy-done.7), kind=kLoop, calls=%fused_computation.36 | loop fusion | flops 4423440 | bytes 6882240 | tf_op jit(solution)/shard_map/reduce_sum | solution.py:34
  120.3 1.7 %collective-permute-done.3 = bf16[2,80,2048]{2,1,0:T(8,128)(2,1)S(1)} collective-permute-done((bf16[2,80,2048]{2,1,0:T(8,128)(2,1)S(1)}, bf16[2,80,2048]{2,1,0:T(8,128)(2,1)S(1)}, u32[]{:S(2)}, u32[]{:S(2)}) %collective-permute-start.3) | collective-permute-done | bytes 655392 | tf_op jit(solution)/shard_map/ppermute | solution.py:151
  123.8 15.9 %collective-permute-done.4 = bf16[2,80,2048]{2,1,0:T(8,128)(2,1)S(1)} collective-permute-done((bf16[2,80,2048]{2,1,0:T(8,128)(2,1)S(1)}, bf16[2,80,2048]{2,1,0:T(8,128)(2,1)S(1)}, u32[]{:S(2)}, u32[]{:S(2)}) %collective-permute-start.4) | collective-permute-done | bytes 655392 | tf_op jit(solution)/shard_map/ppermute | solution.py:152
  142.0 2.6 %convolution_multiply_fusion = f32[2,80,2048]{2,1,0:T(8,128)S(1)} fusion(bf16[2,192,2048]{2,1,0:T(8,128)(2,1)S(1)} %copy-done, f32[2,80]{1,0:T(2,128)S(1)} %select_reduce_fusion, f32[2,80,192]{2,1,0:T(8,128)} %fusion.29, bf16[2,2,2048,192]{2,3,1,0:T(8,128)(2,1)} %param.17, bf16[2,80,2048]{2,1,0:T(8,128)(2,1)S(1)} %add.234, bf16[2,80,2048]{2,1,0:T(8,128)(2,1)} %copy-done.11), kind=kOutput, calls=%fused_computation.34 | convolution fusion | flops 252497920 | bytes 5931648 | tf_op jit(solution)/shard_map/ekf,efd->ekd/dot_general | solution.py:156
  145.9 2.7 %collective-permute-done.5 = f32[2,80,2048]{2,1,0:T(8,128)S(1)} collective-permute-done((f32[2,80,2048]{2,1,0:T(8,128)S(1)}, f32[2,80,2048]{2,1,0:T(8,128)S(1)}, u32[]{:S(2)}, u32[]{:S(2)}) %collective-permute-start.5) | collective-permute-done | bytes 1310752 | tf_op jit(solution)/shard_map/ppermute | solution.py:158
  150.1 16.2 %collective-permute-done.6 = bf16[2,80,2048]{2,1,0:T(8,128)(2,1)S(1)} collective-permute-done((bf16[2,80,2048]{2,1,0:T(8,128)(2,1)S(1)}, bf16[2,80,2048]{2,1,0:T(8,128)(2,1)S(1)}, u32[]{:S(2)}, u32[]{:S(2)}) %collective-permute-start.6) | collective-permute-done | bytes 655392 | tf_op jit(solution)/shard_map/ppermute | solution.py:159
  166.3 3.1 %fusion.20 = bf16[240,2048]{1,0:T(8,128)(2,1)} fusion(bf16[240,2048]{1,0:T(8,128)(2,1)S(1)} %copy-done.2, f32[2,80,2048]{2,1,0:T(8,128)S(1)} %get-tuple-element.10, bf16[2,80,2048]{2,1,0:T(8,128)(2,1)S(1)} %collective-permute-done.6, pred[2,80,960]{2,1,0:T(8,128)(4,1)} %copy-done.12, s32[]{:T(128)S(6)} %select_n.22), kind=kOutput, calls=%fused_computation.33 | convolution fusion | flops 945848320 | bytes 3973124 | tf_op jit(solution)/shard_map/ekt,ekd->td/dot_general | solution.py:162
  (110 shorter events, 32.6 us)
Async XLA Ops:
  0.0 142.0 %copy-start = (bf16[2,192,2048]{2,1,0:T(8,128)(2,1)S(1)}, bf16[2,192,2048]{2,1,0:T(8,128)(2,1)}, u32[]{:S(2)}) copy-start(bf16[2,192,2048]{2,1,0:T(8,128)(2,1)} %param.18) | copy-start | bytes 4718596
  0.0 22.5 %copy-start.6 = (bf16[960,1024]{1,0:T(8,128)(2,1)S(1)}, bf16[960,1024]{1,0:T(8,128)(2,1)}, u32[]{:S(2)}) copy-start(bf16[960,1024]{1,0:T(8,128)(2,1)} %param.11) | copy-start | bytes 5898244
  22.5 0.9 copy-start.5
  22.8 1.7 %copy-start.17 = (s32[1,720]{1,0:T(1,128)S(1)}, s32[1,720]{1,0:T(1,128)}, u32[]{:S(2)}) copy-start(s32[1,720]{1,0:T(1,128)} %get-tuple-element.57) | copy-start | bytes 8644
  22.8 1.7 %copy-start.18 = (s32[1,720]{1,0:T(1,128)S(1)}, s32[1,720]{1,0:T(1,128)}, u32[]{:S(2)}) copy-start(s32[1,720]{1,0:T(1,128)} %get-tuple-element.58) | copy-start | bytes 8644
  22.8 2.3 %copy-start.19 = (s32[1,720]{1,0:T(1,128)S(1)}, s32[1,720]{1,0:T(1,128)}, u32[]{:S(2)}) copy-start(s32[1,720]{1,0:T(1,128)} %stack.104) | copy-start | bytes 8644
  22.8 2.3 %copy-start.20 = (s32[1,720]{1,0:T(1,128)S(1)}, s32[1,720]{1,0:T(1,128)}, u32[]{:S(2)}) copy-start(s32[1,720]{1,0:T(1,128)} %stack.103) | copy-start | bytes 8644
  22.8 3.0 %copy-start.23 = (f32[64]{0:T(128)S(1)}, f32[64]{0:T(128)}, u32[]{:S(2)}) copy-start(f32[64]{0:T(128)} %multiply_power_fusion) | copy-start | bytes 772
  46.2 10.5 %copy-start.21 = (s32[240]{0:T(256)S(1)}, s32[240]{0:T(256)}, u32[]{:S(2)}) copy-start(s32[240]{0:T(256)} %get-tuple-element.35) | copy-start | bytes 2884
  46.2 10.5 %copy-start.22 = (s32[240]{0:T(256)S(1)}, s32[240]{0:T(256)}, u32[]{:S(2)}) copy-start(s32[240]{0:T(256)} %get-tuple-element.38) | copy-start | bytes 2884
  50.5 1.9 %copy-start.3 = (f32[2,240,2048]{2,1,0:T(8,128)}, f32[2,240,2048]{2,1,0:T(8,128)S(1)}, u32[]{:S(2)}) copy-start(f32[2,240,2048]{2,1,0:T(8,128)S(1)} %convolution_bitcast_fusion.1) | copy-start | bytes 11796484
  53.5 13.0 %collective-permute-start = (bf16[240,2048]{1,0:T(8,128)(2,1)}, bf16[240,2048]{1,0:T(8,128)(2,1)}, u32[]{:S(2)}, u32[]{:S(2)}) collective-permute-start(bf16[240,2048]{1,0:T(8,128)(2,1)} %fusion.43), channel_id=1, source_target_pairs={{0,1},{1,0},{2,3},{3,2},{4,5},{5,4},{6,7},{7,6},{8,9},{9,8},{10,11... | collective-permute-start | bytes 2949128 | tf_op jit(solution)/shard_map/ppermute | solution.py:121
  69.9 46.2 %collective-permute-start.2 = (f32[240,2048]{1,0:T(8,128)}, f32[240,2048]{1,0:T(8,128)}, u32[]{:S(2)}, u32[]{:S(2)}) collective-permute-start(f32[240,2048]{1,0:T(8,128)} %fusion.28), channel_id=1, source_target_pairs={{0,2},{1,3},{2,0},{3,1},{4,6},{5,7},{6,4},{7,5},{8,10},{9,11},{10,... | collective-permute-start | bytes 5898248 | tf_op jit(solution)/shard_map/ppermute | solution.py:124
  71.1 0.9 copy-start.8
  71.2 1.1 copy-start.9
  72.2 0.7 copy-start.16
  88.2 7.5 %copy-start.13 = (s32[960,8]{0,1:T(8,128)S(1)}, s32[960,8]{0,1:T(8,128)}, u32[]{:S(2)}) copy-start(s32[960,8]{0,1:T(8,128)} %param.20) | copy-start | bytes 92164
  92.5 1.9 %copy-start.4 = (f32[2,240,2048]{2,1,0:T(8,128)}, f32[2,240,2048]{2,1,0:T(8,128)S(1)}, u32[]{:S(2)}) copy-start(f32[2,240,2048]{2,1,0:T(8,128)S(1)} %convolution_bitcast_fusion) | copy-start | bytes 11796484
  94.4 21.7 %copy-start.7 = (bf16[240,2048]{1,0:T(8,128)(2,1)S(1)}, bf16[240,2048]{1,0:T(8,128)(2,1)}, u32[]{:S(2)}) copy-start(bf16[240,2048]{1,0:T(8,128)(2,1)} %param.14) | copy-start | bytes 2949124
  95.5 4.0 %collective-permute-start.1 = (bf16[240,2048]{1,0:T(8,128)(2,1)}, bf16[240,2048]{1,0:T(8,128)(2,1)S(1)}, u32[]{:S(2)}, u32[]{:S(2)}) collective-permute-start(bf16[240,2048]{1,0:T(8,128)(2,1)} %fusion.44), channel_id=1, source_target_pairs={{0,1},{1,0},{2,3},{3,2},{4,5},{5,4},{6,7},{7,6},{8,9},{9,8},{10,11... | collective-permute-start | bytes 2949128 | tf_op jit(solution)/shard_map/ppermute | solution.py:126
  99.4 19.5 %copy-start.12 = (pred[2,80,960]{2,1,0:T(8,128)(4,1)}, pred[2,80,960]{2,1,0:T(8,128)(4,1)S(1)}, u32[]{:S(2)}) copy-start(pred[2,80,960]{2,1,0:T(8,128)(4,1)S(1)} %fusion.51) | copy-start | bytes 460804
  99.4 19.5 %copy-start.24 = (f32[2048]{0:T(1024)S(1)}, f32[2048]{0:T(1024)}, u32[]{:S(2)}) copy-start(f32[2048]{0:T(1024)} %param.16) | copy-start | bytes 24580
  118.8 21.0 %copy-start.1 = (bf16[240,2048]{1,0:T(8,128)(2,1)}, bf16[240,2048]{1,0:T(8,128)(2,1)S(1)}, u32[]{:S(2)}) copy-start(bf16[240,2048]{1,0:T(8,128)(2,1)S(1)} %get-tuple-element.12) | copy-start | bytes 2949124
  118.8 4.7 %copy-start.14 = (s32[960,8]{0,1:T(8,128)S(1)}, s32[960,8]{0,1:T(8,128)}, u32[]{:S(2)}) copy-start(s32[960,8]{0,1:T(8,128)} %param.20) | copy-start | bytes 92164
  118.8 4.7 %copy-start.15 = (f32[960,8]{0,1:T(8,128)S(1)}, f32[960,8]{0,1:T(8,128)}, u32[]{:S(2)}) copy-start(f32[960,8]{0,1:T(8,128)} %param.21) | copy-start | bytes 92164
  118.8 21.8 %copy-start.10 = (bf16[2,2,2048,192]{2,3,1,0:T(8,128)(2,1)S(1)}, bf16[2,2,2048,192]{2,3,1,0:T(8,128)(2,1)}, u32[]{:S(2)}) copy-start(bf16[2,2,2048,192]{2,3,1,0:T(8,128)(2,1)} %param.17) | copy-start | bytes 9437188
  119.4 2.7 %collective-permute-start.3 = (bf16[2,80,2048]{2,1,0:T(8,128)(2,1)S(1)}, bf16[2,80,2048]{2,1,0:T(8,128)(2,1)S(1)}, u32[]{:S(2)}, u32[]{:S(2)}) collective-permute-start(bf16[2,80,2048]{2,1,0:T(8,128)(2,1)S(1)} %convolution_convert_fusion), channel_id=1, source_target_pairs={{0,1},{1,0},{2,3},{3,2},{4,5},{5,4},{6,7},{7,6},{8,9},{9,8},{10,11... | collective-permute-start | bytes 1966088 | tf_op jit(solution)/shard_map/ppermute | solution.py:151
  122.3 17.5 %collective-permute-start.4 = (bf16[2,80,2048]{2,1,0:T(8,128)(2,1)S(1)}, bf16[2,80,2048]{2,1,0:T(8,128)(2,1)S(1)}, u32[]{:S(2)}, u32[]{:S(2)}) collective-permute-start(bf16[2,80,2048]{2,1,0:T(8,128)(2,1)S(1)} %add.234), channel_id=1, source_target_pairs={{0,2},{1,3},{2,0},{3,1},{4,6},{5,7},{6,4},{7,5},{8,10},{9,11},{10,... | collective-permute-start | bytes 1966088 | tf_op jit(solution)/shard_map/ppermute | solution.py:152
  139.8 0.9 copy-start.11
  144.6 21.7 %copy-start.2 = (bf16[240,2048]{1,0:T(8,128)(2,1)S(1)}, bf16[240,2048]{1,0:T(8,128)(2,1)}, u32[]{:S(2)}) copy-start(bf16[240,2048]{1,0:T(8,128)(2,1)} %copy-done.1) | copy-start | bytes 2949124
  144.6 4.0 %collective-permute-start.5 = (f32[2,80,2048]{2,1,0:T(8,128)S(1)}, f32[2,80,2048]{2,1,0:T(8,128)S(1)}, u32[]{:S(2)}, u32[]{:S(2)}) collective-permute-start(f32[2,80,2048]{2,1,0:T(8,128)S(1)} %convolution_multiply_fusion), channel_id=1, source_target_pairs={{0,1},{1,0},{2,3},{3,2},{4,5},{5,4},{6,7},{7,6},{8,9},{9,8},{10,11... | collective-permute-start | bytes 3932168 | tf_op jit(solution)/shard_map/ppermute | solution.py:158
  148.8 17.5 %collective-permute-start.6 = (bf16[2,80,2048]{2,1,0:T(8,128)(2,1)S(1)}, bf16[2,80,2048]{2,1,0:T(8,128)(2,1)S(1)}, u32[]{:S(2)}, u32[]{:S(2)}) collective-permute-start(bf16[2,80,2048]{2,1,0:T(8,128)(2,1)S(1)} %get-tuple-element.9), channel_id=1, source_target_pairs={{0,2},{1,3},{2,0},{3,1},{4,6},{5,7},{6,4},{7,5},{8,10},{9,11},{10,... | collective-permute-start | bytes 1966088 | tf_op jit(solution)/shard_map/ppermute | solution.py:159
where the time goes:
time: 170 us; the launch traced here: 169 us
  waiting for transfers between devices  53.2 us (31%)
  matrix products  47.1 us (28%)
  local copies, waits for them, and re-layouts  33.3 us (20%)
  other arithmetic  25.8 us (15%)
  starting transfers between devices  9.51 us (6%)
    dot_general x2, matrix products, attend_blocks(): jnp.einsum('nqk,nkd->nqd', weights, value_one, preferred_element_type=jnp...  18.1 us
    ppermute x1, waiting for transfers between devices, local(): from_across = lax.ppermute(across, 'tp', xor_pairs(size, 2))  16.6 us
    ppermute x1, waiting for transfers between devices, local(): lax.ppermute(scaled.astype(jnp.bfloat16), 'tp', xor_pairs(size, 2))  16.2 us
    ppermute x1, waiting for transfers between devices, local(): picked = picked + lax.ppermute(picked, 'tp', xor_pairs(size, 2))  15.9 us
    sub x2, matrix products, attend_blocks(): weights = jnp.exp(scores - peak)  13 us
    unnamed x55, local copies, waits for them, and re-layouts  8.55 us
    dot_general x2, matrix products, projected_blocks(): jnp.einsum('nrhc,hcd->nrd', attended, out_weight.reshape(attended.shape[2...  8.49 us
    dynamic_slice x4, local copies, waits for them, and re-layouts, attend_blocks(): lax.dynamic_slice_in_dim(keys_after_rotary, s, span)  6.96 us
  transfers between devices with their start and end apart: 7, of which 5 were waited for; matrix products, arithmetic and copies ran while one was open for 21% of the time, Pallas kernels for 0%

commit v1 on v0

--- a/solution.py
+++ b/solution.py
@@ -120,8 +120,14 @@
     first_pair = projected_blocks([me ^ 3, me ^ 2], query_heads)
     partner_cross = lax.ppermute(first_pair[0].astype(jnp.bfloat16), "tp", xor_pairs(size, 1))
     across = first_pair[1] + partner_cross.astype(jnp.float32)
-    across, later_queries = lax.optimization_barrier((across, query_heads))
-    from_across = lax.ppermute(across, "tp", xor_pairs(size, 2))
+    high = across.astype(jnp.bfloat16)
+    half = across.shape[1] // 2
+    low = (across[:, :half] - high[:, :half].astype(jnp.float32)).astype(jnp.bfloat16)
+    message, later_queries = lax.optimization_barrier(
+        (jnp.concatenate([high, low], axis=1), query_heads)
+    )
+    message = lax.ppermute(message, "tp", xor_pairs(size, 2)).astype(jnp.float32)
+    from_across = message[:, : 2 * half] + jnp.pad(message[:, 2 * half :], ((0, 0), (0, half)))
     second_pair = projected_blocks([me ^ 1, me], later_queries)
     partner_own = lax.ppermute(second_pair[0].astype(jnp.bfloat16), "tp", xor_pairs(size, 1))
     projected = (

time: 170 us -> 155 us (0.912)
  waiting for transfers between devices: 53.2 us -> 42.6 us
  other arithmetic: 25.8 us -> 22.5 us
  local copies, waits for them, and re-layouts: 33.3 us -> 31 us
    ppermute x1, waiting for transfers between devices: 16.6 us -> 6.07 us  [local(): lax.ppermute(message, 'tp', xor_pairs(size, 2)).astype(jnp.float32)]
    add x1 -> x0, other arithmetic: 3.39 us -> none  [local(): across = first_pair[1] + partner_cross.astype(jnp.float32)]
    convert_element_type x0 -> x3, other arithmetic: none -> 2.34 us  [the longest x1 1.87 us: local(): high = across.astype(jnp.bfloat16)]
    unnamed x55 -> x65, local copies, waits for them, and re-layouts: 8.55 us -> 10.4 us
  transfers between devices with their start and end apart: 7 -> 7, of which waited for: 5 -> 5; matrix products, arithmetic and copies ran while one was open for 21% -> 24% of each run, Pallas kernels for 0% -> 0%
where the time goes in v1:
time: 155 us; the launch traced here: 154 us
  matrix products  46.7 us (30%)
  waiting for transfers between devices  42.6 us (27%)
  local copies, waits for them, and re-layouts  31 us (20%)
  other arithmetic  22.5 us (15%)
  starting transfers between devices  10.7 us (7%)
    dot_general x2, matrix products, attend_blocks(): jnp.einsum('nqk,nkd->nqd', weights, value_one, preferred_element_type=jnp...  18 us
    ppermute x1, waiting for transfers between devices, local(): lax.ppermute(scaled.astype(jnp.bfloat16), 'tp', xor_pairs(size, 2))  16.2 us
    ppermute x1, waiting for transfers between devices, local(): picked = picked + lax.ppermute(picked, 'tp', xor_pairs(size, 2))  15.9 us
    sub x2, matrix products, attend_blocks(): weights = jnp.exp(scores - peak)  12.8 us
    unnamed x65, local copies, waits for them, and re-layouts  10.4 us
    dot_general x2, matrix products, projected_blocks(): jnp.einsum('nrhc,hcd->nrd', attended, out_weight.reshape(attended.shape[2...  8.47 us
    dynamic_slice x4, local copies, waits for them, and re-layouts, attend_blocks(): lax.dynamic_slice_in_dim(keys_after_rotary, s, span)  6.93 us
    ppermute x1, waiting for transfers between devices, local(): lax.ppermute(message, 'tp', xor_pairs(size, 2)).astype(jnp.float32)  6.07 us
  transfers between devices with their start and end apart: 7, of which 5 were waited for; matrix products, arithmetic and copies ran while one was open for 24% of the time, Pallas kernels for 0%

profile of v1, /device:TPU:1, one launch (start us, length us, event | category | flops | bytes accessed | tf_op | source)
XLA Modules:
  0.0 154.1 jit_solution(2486120256445708994)
XLA Ops:
  1.9 1.5 fusion.124
  7.8 1.9 %copy.31 = bf16[960,128]{0,1:T(8,128)(2,1)} copy(bf16[960,128]{1,0:T(8,128)(2,1)} %param.12) | data formatting | bytes 491520 | tf_op args[1]
  10.8 1.7 %fusion.66 = (bf16[960,1,64]{0,2,1:T(8,128)(2,1)S(1)}, bf16[960,1,64]{0,2,1:T(8,128)(2,1)S(1)}) fusion(f32[960,1,128]{0,2,1:T(8,128)S(1)} %bitcast_convert_fusion, f32[64]{0:T(128)} %multiply_power_fusion, f32[960]{0:T(1024)S(1)} %get-tuple-element.46), kind=kLoop, calls=%fused_computation.111 | loop fusion | flops 552960 | bytes 741376 | tf_op jit(solution)/shard_map/convert.13
  12.5 1.4 fusion.74
  13.9 1.7 %copy.33 = bf16[720,1,128]{2,0,1:T(8,128)(2,1)} copy(bf16[720,1,128]{0,2,1:T(8,128)(2,1)} %get-tuple-element.27) | data formatting | bytes 368640 | tf_op jit(solution)/shard_map/dynamic_slice | solution.py:54
  15.6 1.7 %copy.32 = bf16[720,1,128]{2,0,1:T(8,128)(2,1)} copy(bf16[720,1,128]{0,2,1:T(8,128)(2,1)} %get-tuple-element.26) | data formatting | bytes 368640 | tf_op jit(solution)/shard_map/dynamic_slice | solution.py:54
  20.9 2.6 %multiply_cosine_fusion.1 = (f32[480,64]{1,0:T(8,128)}, f32[480,64]{1,0:T(8,128)}, f32[480,64]{1,0:T(8,128)S(1)}, f32[480,64]{1,0:T(8,128)S(1)}) fusion(f32[480]{0:T(512)S(1)} %get-tuple-element.58, f32[64]{0:T(128)S(1)} %copy-done.28, f32[480]{0:T(512)S(1)} %get-tuple-element.57), kind=kLoop, calls=%fused_computation.105 | loop fusion | flops 61440 | bytes 495616 | tf_op jit(solution)/shard_map/cos | solution.py:23
  24.2 6.6 %fusion.126 = f32[2,1920]{1,0:T(2,128)} fusion(s32[2,1920]{1,0:T(2,128)} %le.35, s32[2,720]{1,0:T(2,128)} %pad_add_fusion.3, s32[2,720]{1,0:T(2,128)} %pad_add_fusion.2, s32[2,1920]{1,0:T(2,128)} %eq.60, bf16[1,720,128]{2,1,0:T(8,128)(2,1)} %bitcast.112, bf16[1,720,128]{2,1,0:T(8,128)(2,1)} %bitcast.114, bf16[2,1920,64]{2,1,0:T(8,128)(2,1)S(1)} %bitcast.110, ...), kind=kOutput, calls=%fused_computation.190 | convolution fusion | flops 729293504 | bytes 1409280 | tf_op jit(solution)/shard_map/sub | solution.py:76
  30.8 8.9 %fusion.39 = bf16[2,240,8,128]{3,2,1,0:T(8,128)(2,1)} fusion(f32[2,1920]{1,0:T(2,128)} %fusion.126, bf16[1,720,128]{2,1,0:T(8,128)(2,1)} %get-tuple-element.30, bf16[1,720,128]{2,1,0:T(8,128)(2,1)} %get-tuple-element.31, s32[2,1920]{1,0:T(2,128)} %le.35, s32[2,720]{1,0:T(2,128)} %pad_add_fusion.3, s32[2,720]{1,0:T(2,128)} %pad_add_fusion.2, ...), kind=kOutput, calls=%fused_computation.64 | convolution fusion | flops 1440526848 | bytes 2760960 | tf_op jit(solution)/shard_map/nqk,nkd->nqd/dot_general | solution.py:78
  39.6 4.2 %convolution_bitcast_fusion.1 = f32[2,240,2048]{2,1,0:T(8,128)S(1)} fusion(bf16[8,128,2048,1]{2,1,0,3:T(8,128)(2,1)} %bitcast.131, bf16[2,240,8,128]{3,2,1,0:T(8,128)(2,1)} %fusion.39), kind=kOutput, calls=%fused_computation.26 | convolution fusion | flops 2013265920 | bytes 9109504 | tf_op jit(solution)/shard_map/nrhc,hcd->nrd/dot_general | solution.py:115
  43.9 1.8 %copy-done.3 = f32[2,240,2048]{2,1,0:T(8,128)} copy-done((f32[2,240,2048]{2,1,0:T(8,128)}, f32[2,240,2048]{2,1,0:T(8,128)S(1)}, u32[]{:S(2)}) %copy-start.3) | copy-done | bytes 3932184
  45.9 3.3 %collective-permute-start = (bf16[240,2048]{1,0:T(8,128)(2,1)S(1)}, bf16[240,2048]{1,0:T(8,128)(2,1)S(1)}, u32[]{:S(2)}, u32[]{:S(2)}) collective-permute-start(bf16[240,2048]{1,0:T(8,128)(2,1)S(1)} %fusion.43), channel_id=1, source_target_pairs={{0,1},{1,0},{2,3},{3,2},{4,5},{5,4},{6,7},{7,6},{8,9},{9,8},{10,11... | collective-permute-start | bytes 2949128 | tf_op jit(solution)/shard_map/ppermute | solution.py:121
  50.0 1.7 %le.31 = s32[2,1920]{1,0:T(2,128)} reshape(s32[2,240,8]{2,1,0:T(8,128)} %broadcast_in_dim.30) | data formatting | bytes 30720 | tf_op jit(solution)/shard_map/le | solution.py:72
  54.8 1.7 %copy.36 = bf16[720,1,128]{2,0,1:T(8,128)(2,1)} copy(bf16[720,1,128]{0,2,1:T(8,128)(2,1)} %get-tuple-element.28) | data formatting | bytes 368640 | tf_op jit(solution)/shard_map/dynamic_slice | solution.py:54
  56.5 1.7 %copy.35 = bf16[720,1,128]{2,0,1:T(8,128)(2,1)} copy(bf16[720,1,128]{0,2,1:T(8,128)(2,1)} %get-tuple-element.25) | data formatting | bytes 368640 | tf_op jit(solution)/shard_map/dynamic_slice | solution.py:54
  60.2 1.9 %fusion.121 = (bf16[240,2048]{1,0:T(8,128)(2,1)S(1)}, f32[240,2048]{1,0:T(8,128)S(1)}) fusion(bf16[240,2048]{1,0:T(8,128)(2,1)S(1)} %collective-permute-done, f32[2,240,2048]{2,1,0:T(8,128)} %copy-done.3), kind=kLoop, calls=%fused_computation.186 | loop fusion | flops 1474560 | bytes 5898240 | tf_op jit(solution)/shard_map/convert_element_type | solution.py:123
  66.0 2.0 %subtract_convert_fusion = (bf16[480,8,64]{2,1,0:T(8,128)(2,1)}, bf16[480,8,64]{2,1,0:T(8,128)(2,1)}) fusion(f32[480,8,128]{2,1,0:T(8,128)S(1)} %bitcast.103, f32[480,64]{1,0:T(8,128)S(1)} %copy-done.11, f32[480,64]{1,0:T(8,128)S(1)} %copy-done.10), kind=kLoop, calls=%fused_computation.52 | loop fusion | flops 1966080 | bytes 3194880 | tf_op jit(solution)/shard_map/convert.10
  68.1 6.2 %fusion.127 = f32[2,1920]{1,0:T(2,128)S(1)} fusion(s32[2,1920]{1,0:T(2,128)S(1)} %copy-done.19, s32[2,720]{1,0:T(2,128)S(1)} %copy-done.24, s32[2,720]{1,0:T(2,128)S(1)} %copy-done.25, s32[2,1920]{1,0:T(2,128)S(1)} %eq.56, bf16[1,720,128]{2,1,0:T(8,128)(2,1)} %bitcast.116, bf16[1,720,128]{2,1,0:T(8,128)(2,1)} %bitcast.118, ...), kind=kOutput, calls=%fused_computation.191 | convolution fusion | flops 729293504 | bytes 1409280 | tf_op jit(solution)/shard_map/sub | solution.py:76
  74.3 9.1 %fusion.40 = bf16[2,240,8,128]{3,2,1,0:T(8,128)(2,1)} fusion(f32[2,1920]{1,0:T(2,128)S(1)} %fusion.127, bf16[1,720,128]{2,1,0:T(8,128)(2,1)S(1)} %copy-done.16, bf16[1,720,128]{2,1,0:T(8,128)(2,1)S(1)} %copy-done.15, s32[2,1920]{1,0:T(2,128)S(1)} %copy-done.19, s32[2,720]{1,0:T(2,128)S(1)} %copy-done.24, s32[2,720]{1,0:T(2,128)S(1)} %copy-done.25, ...), kind=kOutput, calls=%fused_computation.65 | convolution fusion | flops 1440526848 | bytes 2760960 | tf_op jit(solution)/shard_map/nqk,nkd->nqd/dot_general | solution.py:78
  83.4 4.2 %convolution_bitcast_fusion = f32[2,240,2048]{2,1,0:T(8,128)S(1)} fusion(bf16[8,128,2048,1]{2,1,0,3:T(8,128)(2,1)} %bitcast.132, bf16[2,240,8,128]{3,2,1,0:T(8,128)(2,1)} %fusion.40), kind=kOutput, calls=%fused_computation.25 | convolution fusion | flops 2013265920 | bytes 9109504 | tf_op jit(solution)/shard_map/nrhc,hcd->nrd/dot_general | solution.py:115
  87.7 1.8 %copy-done.5 = f32[2,240,2048]{2,1,0:T(8,128)} copy-done((f32[2,240,2048]{2,1,0:T(8,128)}, f32[2,240,2048]{2,1,0:T(8,128)S(1)}, u32[]{:S(2)}) %copy-start.5) | copy-done | bytes 3932184
  92.6 6.1 %collective-permute-done.2 = bf16[240,3072]{1,0:T(8,128)(2,1)S(1)} collective-permute-done((bf16[240,3072]{1,0:T(8,128)(2,1)}, bf16[240,3072]{1,0:T(8,128)(2,1)S(1)}, u32[]{:S(2)}, u32[]{:S(2)}) %collective-permute-start.2) | collective-permute-done | bytes 1474592 | tf_op jit(solution)/shard_map/ppermute | solution.py:129
  101.1 1.8 %fusion.21 = (f32[240]{0:T(256)S(1)}, bf16[240,2048]{1,0:T(8,128)(2,1)S(1)}) fusion(f32[240,1024]{1,0:T(8,128)S(1)} %slice.91, f32[240,3072]{1,0:T(8,128)S(1)} %convert_element_type.149, bf16[240,2048]{1,0:T(8,128)(2,1)} %collective-permute-done.1, f32[2,240,2048]{2,1,0:T(8,128)S(1)} %copy-done.6, bf16[240,2048]{1,0:T(8,128)(2,1)S(1)} %copy-done.9), kind=kLoop, calls=%fused_computation.36 | loop fusion | flops 4914960 | bytes 7865280 | tf_op jit(solution)/shard_map/reduce_sum | solution.py:34
  103.5 1.3 collective-permute-start.3
  104.8 1.7 %collective-permute-done.3 = bf16[2,80,2048]{2,1,0:T(8,128)(2,1)S(1)} collective-permute-done((bf16[2,80,2048]{2,1,0:T(8,128)(2,1)S(1)}, bf16[2,80,2048]{2,1,0:T(8,128)(2,1)S(1)}, u32[]{:S(2)}, u32[]{:S(2)}) %collective-permute-start.3) | collective-permute-done | bytes 655392 | tf_op jit(solution)/shard_map/ppermute | solution.py:157
  106.7 1.6 %collective-permute-start.4 = (bf16[2,80,2048]{2,1,0:T(8,128)(2,1)S(1)}, bf16[2,80,2048]{2,1,0:T(8,128)(2,1)S(1)}, u32[]{:S(2)}, u32[]{:S(2)}) collective-permute-start(bf16[2,80,2048]{2,1,0:T(8,128)(2,1)S(1)} %add.240), channel_id=1, source_target_pairs={{0,2},{1,3},{2,0},{3,1},{4,6},{5,7},{6,4},{7,5},{8,10},{9,11},{10,... | collective-permute-start | bytes 1966088 | tf_op jit(solution)/shard_map/ppermute | solution.py:158
  108.6 15.9 %collective-permute-done.4 = bf16[2,80,2048]{2,1,0:T(8,128)(2,1)S(1)} collective-permute-done((bf16[2,80,2048]{2,1,0:T(8,128)(2,1)S(1)}, bf16[2,80,2048]{2,1,0:T(8,128)(2,1)S(1)}, u32[]{:S(2)}, u32[]{:S(2)}) %collective-permute-start.4) | collective-permute-done | bytes 655392 | tf_op jit(solution)/shard_map/ppermute | solution.py:158
  125.4 1.3 fusion.29
  126.7 2.6 %convolution_multiply_fusion = f32[2,80,2048]{2,1,0:T(8,128)S(1)} fusion(bf16[2,192,2048]{2,1,0:T(8,128)(2,1)S(1)} %copy-done, f32[2,80]{1,0:T(2,128)S(1)} %select_reduce_fusion, f32[2,80,192]{2,1,0:T(8,128)} %fusion.29, bf16[2,2,2048,192]{2,3,1,0:T(8,128)(2,1)} %param.17, bf16[2,80,2048]{2,1,0:T(8,128)(2,1)S(1)} %add.240, bf16[2,80,2048]{2,1,0:T(8,128)(2,1)} %copy-done.13), kind=kOutput, calls=%fused_computation.34 | convolution fusion | flops 252497920 | bytes 5931648 | tf_op jit(solution)/shard_map/ekf,efd->ekd/dot_general | solution.py:162
  130.6 2.7 %collective-permute-done.5 = f32[2,80,2048]{2,1,0:T(8,128)S(1)} collective-permute-done((f32[2,80,2048]{2,1,0:T(8,128)S(1)}, f32[2,80,2048]{2,1,0:T(8,128)S(1)}, u32[]{:S(2)}, u32[]{:S(2)}) %collective-permute-start.5) | collective-permute-done | bytes 1310752 | tf_op jit(solution)/shard_map/ppermute | solution.py:164
  134.8 16.2 %collective-permute-done.6 = bf16[2,80,2048]{2,1,0:T(8,128)(2,1)S(1)} collective-permute-done((bf16[2,80,2048]{2,1,0:T(8,128)(2,1)S(1)}, bf16[2,80,2048]{2,1,0:T(8,128)(2,1)S(1)}, u32[]{:S(2)}, u32[]{:S(2)}) %collective-permute-start.6) | collective-permute-done | bytes 655392 | tf_op jit(solution)/shard_map/ppermute | solution.py:165
  151.0 3.1 %fusion.20 = bf16[240,2048]{1,0:T(8,128)(2,1)} fusion(bf16[240,2048]{1,0:T(8,128)(2,1)S(1)} %copy-done.2, f32[2,80,2048]{2,1,0:T(8,128)S(1)} %get-tuple-element.10, bf16[2,80,2048]{2,1,0:T(8,128)(2,1)S(1)} %collective-permute-done.6, pred[2,80,960]{2,1,0:T(8,128)(4,1)} %copy-done.14, s32[]{:T(128)S(6)} %select_n.22), kind=kOutput, calls=%fused_computation.33 | convolution fusion | flops 945848320 | bytes 3973124 | tf_op jit(solution)/shard_map/ekt,ekd->td/dot_general | solution.py:168
  (124 shorter events, 31.4 us)
Async XLA Ops:
  0.0 126.7 %copy-start = (bf16[2,192,2048]{2,1,0:T(8,128)(2,1)S(1)}, bf16[2,192,2048]{2,1,0:T(8,128)(2,1)}, u32[]{:S(2)}) copy-start(bf16[2,192,2048]{2,1,0:T(8,128)(2,1)} %param.18) | copy-start | bytes 4718596
  7.8 9.5 %copy-start.7 = (bf16[960,1024]{1,0:T(8,128)(2,1)S(1)}, bf16[960,1024]{1,0:T(8,128)(2,1)}, u32[]{:S(2)}) copy-start(bf16[960,1024]{1,0:T(8,128)(2,1)} %param.11) | copy-start | bytes 5898244
  17.7 1.9 %copy-start.20 = (s32[1,720]{1,0:T(1,128)S(1)}, s32[1,720]{1,0:T(1,128)}, u32[]{:S(2)}) copy-start(s32[1,720]{1,0:T(1,128)} %get-tuple-element.59) | copy-start | bytes 8644
  17.7 1.9 %copy-start.21 = (s32[1,720]{1,0:T(1,128)S(1)}, s32[1,720]{1,0:T(1,128)}, u32[]{:S(2)}) copy-start(s32[1,720]{1,0:T(1,128)} %get-tuple-element.60) | copy-start | bytes 8644
  17.7 2.5 %copy-start.22 = (s32[1,720]{1,0:T(1,128)S(1)}, s32[1,720]{1,0:T(1,128)}, u32[]{:S(2)}) copy-start(s32[1,720]{1,0:T(1,128)} %stack.104) | copy-start | bytes 8644
  17.7 2.5 %copy-start.23 = (s32[1,720]{1,0:T(1,128)S(1)}, s32[1,720]{1,0:T(1,128)}, u32[]{:S(2)}) copy-start(s32[1,720]{1,0:T(1,128)} %stack.103) | copy-start | bytes 8644
  17.7 3.2 %copy-start.28 = (f32[64]{0:T(128)S(1)}, f32[64]{0:T(128)}, u32[]{:S(2)}) copy-start(f32[64]{0:T(128)} %multiply_power_fusion) | copy-start | bytes 772
  43.9 1.8 %copy-start.3 = (f32[2,240,2048]{2,1,0:T(8,128)}, f32[2,240,2048]{2,1,0:T(8,128)S(1)}, u32[]{:S(2)}) copy-start(f32[2,240,2048]{2,1,0:T(8,128)S(1)} %convolution_bitcast_fusion.1) | copy-start | bytes 11796484
  45.7 3.4 %copy-start.26 = (s32[240]{0:T(256)S(1)}, s32[240]{0:T(256)}, u32[]{:S(2)}) copy-start(s32[240]{0:T(256)} %get-tuple-element.37) | copy-start | bytes 2884
  45.7 3.4 %copy-start.27 = (s32[240]{0:T(256)S(1)}, s32[240]{0:T(256)}, u32[]{:S(2)}) copy-start(s32[240]{0:T(256)} %get-tuple-element.40) | copy-start | bytes 2884
  45.9 14.3 %collective-permute-start = (bf16[240,2048]{1,0:T(8,128)(2,1)S(1)}, bf16[240,2048]{1,0:T(8,128)(2,1)S(1)}, u32[]{:S(2)}, u32[]{:S(2)}) collective-permute-start(bf16[240,2048]{1,0:T(8,128)(2,1)S(1)} %fusion.43), channel_id=1, source_target_pairs={{0,1},{1,0},{2,3},{3,2},{4,5},{5,4},{6,7},{7,6},{8,9},{9,8},{10,11... | collective-permute-start | bytes 2949128 | tf_op jit(solution)/shard_map/ppermute | solution.py:121
  62.1 2.6 %copy-start.8 = (bf16[960,1024]{1,0:T(8,128)(2,1)S(1)}, bf16[960,1024]{1,0:T(8,128)(2,1)}, u32[]{:S(2)}) copy-start(bf16[960,1024]{1,0:T(8,128)(2,1)} %param.11) | copy-start | bytes 5898244
  63.5 35.2 %collective-permute-start.2 = (bf16[240,3072]{1,0:T(8,128)(2,1)}, bf16[240,3072]{1,0:T(8,128)(2,1)S(1)}, u32[]{:S(2)}, u32[]{:S(2)}) collective-permute-start(bf16[240,3072]{1,0:T(8,128)(2,1)} %pad_maximum_fusion), channel_id=1, source_target_pairs={{0,2},{1,3},{2,0},{3,1},{4,6},{5,7},{6,4},{7,5},{8,10},{9,11},{10,... | collective-permute-start | bytes 4423688 | tf_op jit(solution)/shard_map/ppermute | solution.py:129
  66.0 2.0 %copy-start.19 = (s32[2,1920]{1,0:T(2,128)S(1)}, s32[2,1920]{1,0:T(2,128)}, u32[]{:S(2)}) copy-start(s32[2,1920]{1,0:T(2,128)} %le.31) | copy-start | bytes 46084
  66.0 2.0 %copy-start.24 = (s32[2,720]{1,0:T(2,128)S(1)}, s32[2,720]{1,0:T(2,128)}, u32[]{:S(2)}) copy-start(s32[2,720]{1,0:T(2,128)} %pad_add_fusion.1) | copy-start | bytes 17284
  66.0 2.0 %copy-start.25 = (s32[2,720]{1,0:T(2,128)S(1)}, s32[2,720]{1,0:T(2,128)}, u32[]{:S(2)}) copy-start(s32[2,720]{1,0:T(2,128)} %pad_add_fusion) | copy-start | bytes 17284
  68.1 6.3 %copy-start.15 = (bf16[1,720,128]{2,1,0:T(8,128)(2,1)S(1)}, bf16[1,720,128]{2,1,0:T(8,128)(2,1)}, u32[]{:S(2)}) copy-start(bf16[1,720,128]{2,1,0:T(8,128)(2,1)} %get-tuple-element.29) | copy-start | bytes 552964
  68.1 6.3 %copy-start.16 = (bf16[1,720,128]{2,1,0:T(8,128)(2,1)S(1)}, bf16[1,720,128]{2,1,0:T(8,128)(2,1)}, u32[]{:S(2)}) copy-start(bf16[1,720,128]{2,1,0:T(8,128)(2,1)} %get-tuple-element.32) | copy-start | bytes 552964
  87.7 1.8 %copy-start.5 = (f32[2,240,2048]{2,1,0:T(8,128)}, f32[2,240,2048]{2,1,0:T(8,128)S(1)}, u32[]{:S(2)}) copy-start(f32[2,240,2048]{2,1,0:T(8,128)S(1)} %convolution_bitcast_fusion) | copy-start | bytes 11796484
  89.5 1.8 %copy-start.17 = (s32[960,8]{0,1:T(8,128)S(1)}, s32[960,8]{0,1:T(8,128)}, u32[]{:S(2)}) copy-start(s32[960,8]{0,1:T(8,128)} %param.20) | copy-start | bytes 92164
  90.6 8.5 %collective-permute-start.1 = (bf16[240,2048]{1,0:T(8,128)(2,1)}, bf16[240,2048]{1,0:T(8,128)(2,1)}, u32[]{:S(2)}, u32[]{:S(2)}) collective-permute-start(bf16[240,2048]{1,0:T(8,128)(2,1)} %fusion.44), channel_id=1, source_target_pairs={{0,1},{1,0},{2,3},{3,2},{4,5},{5,4},{6,7},{7,6},{8,9},{9,8},{10,11... | collective-permute-start | bytes 2949128 | tf_op jit(solution)/shard_map/ppermute | solution.py:132
  92.5 10.4 %copy-start.14 = (pred[2,80,960]{2,1,0:T(8,128)(4,1)}, pred[2,80,960]{2,1,0:T(8,128)(4,1)S(1)}, u32[]{:S(2)}) copy-start(pred[2,80,960]{2,1,0:T(8,128)(4,1)S(1)} %fusion.52) | copy-start | bytes 460804
  98.7 2.3 %copy-start.6 = (f32[2,240,2048]{2,1,0:T(8,128)S(1)}, f32[2,240,2048]{2,1,0:T(8,128)}, u32[]{:S(2)}) copy-start(f32[2,240,2048]{2,1,0:T(8,128)} %copy-done.5) | copy-start | bytes 11796484
  99.1 3.9 %copy-start.29 = (f32[2048]{0:T(1024)S(1)}, f32[2048]{0:T(1024)}, u32[]{:S(2)}) copy-start(f32[2048]{0:T(1024)} %param.16) | copy-start | bytes 24580
  102.9 5.4 %copy-start.1 = (bf16[240,2048]{1,0:T(8,128)(2,1)}, bf16[240,2048]{1,0:T(8,128)(2,1)S(1)}, u32[]{:S(2)}) copy-start(bf16[240,2048]{1,0:T(8,128)(2,1)S(1)} %get-tuple-element.12) | copy-start | bytes 2949124
  102.9 5.4 %copy-start.18 = (f32[960,8]{0,1:T(8,128)S(1)}, f32[960,8]{0,1:T(8,128)}, u32[]{:S(2)}) copy-start(f32[960,8]{0,1:T(8,128)} %param.21) | copy-start | bytes 92164
  103.0 22.4 %copy-start.12 = (bf16[2,2,2048,192]{2,3,1,0:T(8,128)(2,1)S(1)}, bf16[2,2,2048,192]{2,3,1,0:T(8,128)(2,1)}, u32[]{:S(2)}) copy-start(bf16[2,2,2048,192]{2,3,1,0:T(8,128)(2,1)} %param.17) | copy-start | bytes 9437188
  103.5 3.1 %collective-permute-start.3 = (bf16[2,80,2048]{2,1,0:T(8,128)(2,1)S(1)}, bf16[2,80,2048]{2,1,0:T(8,128)(2,1)S(1)}, u32[]{:S(2)}, u32[]{:S(2)}) collective-permute-start(bf16[2,80,2048]{2,1,0:T(8,128)(2,1)S(1)} %convolution_convert_fusion), channel_id=1, source_target_pairs={{0,1},{1,0},{2,3},{3,2},{4,5},{5,4},{6,7},{7,6},{8,9},{9,8},{10,11... | collective-permute-start | bytes 1966088 | tf_op jit(solution)/shard_map/ppermute | solution.py:157
  106.7 17.8 %collective-permute-start.4 = (bf16[2,80,2048]{2,1,0:T(8,128)(2,1)S(1)}, bf16[2,80,2048]{2,1,0:T(8,128)(2,1)S(1)}, u32[]{:S(2)}, u32[]{:S(2)}) collective-permute-start(bf16[2,80,2048]{2,1,0:T(8,128)(2,1)S(1)} %add.240), channel_id=1, source_target_pairs={{0,2},{1,3},{2,0},{3,1},{4,6},{5,7},{6,4},{7,5},{8,10},{9,11},{10,... | collective-permute-start | bytes 1966088 | tf_op jit(solution)/shard_map/ppermute | solution.py:158
  129.3 21.7 %copy-start.2 = (bf16[240,2048]{1,0:T(8,128)(2,1)S(1)}, bf16[240,2048]{1,0:T(8,128)(2,1)}, u32[]{:S(2)}) copy-start(bf16[240,2048]{1,0:T(8,128)(2,1)} %copy-done.1) | copy-start | bytes 2949124
  129.3 4.0 %collective-permute-start.5 = (f32[2,80,2048]{2,1,0:T(8,128)S(1)}, f32[2,80,2048]{2,1,0:T(8,128)S(1)}, u32[]{:S(2)}, u32[]{:S(2)}) collective-permute-start(f32[2,80,2048]{2,1,0:T(8,128)S(1)} %convolution_multiply_fusion), channel_id=1, source_target_pairs={{0,1},{1,0},{2,3},{3,2},{4,5},{5,4},{6,7},{7,6},{8,9},{9,8},{10,11... | collective-permute-start | bytes 3932168 | tf_op jit(solution)/shard_map/ppermute | solution.py:164
  133.5 17.5 %collective-permute-start.6 = (bf16[2,80,2048]{2,1,0:T(8,128)(2,1)S(1)}, bf16[2,80,2048]{2,1,0:T(8,128)(2,1)S(1)}, u32[]{:S(2)}, u32[]{:S(2)}) collective-permute-start(bf16[2,80,2048]{2,1,0:T(8,128)(2,1)S(1)} %get-tuple-element.9), channel_id=1, source_target_pairs={{0,2},{1,3},{2,0},{3,1},{4,6},{5,7},{6,4},{7,5},{8,10},{9,11},{10,... | collective-permute-start | bytes 1966088 | tf_op jit(solution)/shard_map/ppermute | solution.py:165
  (5 other events, 5.0 us)

commit v2 on v1

--- a/solution.py
+++ b/solution.py
@@ -154,17 +154,24 @@
         "ekt,td->ekd", select_loc.astype(jnp.bfloat16), normed,
         preferred_element_type=jnp.float32,
     ).astype(jnp.bfloat16)
+    on_core = me % 2
     picked = picked + lax.ppermute(picked, "tp", xor_pairs(size, 1))
-    picked = picked + lax.ppermute(picked, "tp", xor_pairs(size, 2))
+    mine = picked[on_core]
+    mine = mine + lax.ppermute(mine, "tp", xor_pairs(size, 2))
+    other = lax.ppermute(mine, "tp", xor_pairs(size, 1))
+    picked = jnp.where(on_core == 0, jnp.stack([mine, other]), jnp.stack([other, mine]))
     gate = jnp.einsum("ekd,edf->ekf", picked, gate_up[:, 0], preferred_element_type=jnp.float32)
     upward = jnp.einsum("ekd,edf->ekf", picked, gate_up[:, 1], preferred_element_type=jnp.float32)
     active = (jax.nn.silu(gate) * upward).astype(jnp.bfloat16)
     outputs = jnp.einsum("ekf,efd->ekd", active, down_weight, preferred_element_type=jnp.float32)
     scaled = route_sel[:, :, None] * outputs
     scaled = scaled + lax.ppermute(scaled, "tp", xor_pairs(size, 1))
-    scaled = scaled + lax.ppermute(
-        scaled.astype(jnp.bfloat16), "tp", xor_pairs(size, 2)
+    mine = scaled[on_core]
+    mine = mine + lax.ppermute(
+        mine.astype(jnp.bfloat16), "tp", xor_pairs(size, 2)
     ).astype(jnp.float32)
+    other = lax.ppermute(mine, "tp", xor_pairs(size, 1))
+    scaled = jnp.where(on_core == 0, jnp.stack([mine, other]), jnp.stack([other, mine]))
     experts = jnp.einsum(
         "ekt,ekd->td", select_loc.astype(jnp.float32), scaled,
         precision=lax.Precision.HIGHEST, preferred_element_type=jnp.float32,

time: 155 us -> 146 us (0.942)
  waiting for transfers between devices: 42.6 us -> 31.5 us
  starting transfers between devices: 10.7 us -> 12.5 us
    ppermute x2 -> x4, waiting for transfers between devices: 32.1 us -> 21.1 us  [the longest x1 9.18 us: local(): lax.ppermute(mine.astype(jnp.bfloat16), 'tp', xor_pairs(size, 2))]
    ppermute x2 -> x4, starting transfers between devices: 2.87 us -> 5.51 us  [the longest x2 2.89 us: local(): other = lax.ppermute(mine, 'tp', xor_pairs(size, 1))]
    unnamed x65 -> x61, local copies, waits for them, and re-layouts: 10.4 us -> 11.2 us
  transfers between devices with their start and end apart: 7 -> 9, of which waited for: 5 -> 7; matrix products, arithmetic and copies ran while one was open for 24% -> 25% of each run, Pallas kernels for 0% -> 0%
where the time goes in v2:
time: 146 us; the launch traced here: 145 us
  matrix products  46.6 us (32%)
  local copies, waits for them, and re-layouts  31.8 us (22%)
  waiting for transfers between devices  31.5 us (22%)
  other arithmetic  22.5 us (15%)
  starting transfers between devices  12.5 us (9%)
    dot_general x2, matrix products, attend_blocks(): jnp.einsum('nqk,nkd->nqd', weights, value_one, preferred_element_type=jnp...  18 us
    sub x2, matrix products, attend_blocks(): weights = jnp.exp(scores - peak)  12.8 us
    unnamed x61, local copies, waits for them, and re-layouts  11.2 us
    ppermute x1, waiting for transfers between devices, local(): lax.ppermute(mine.astype(jnp.bfloat16), 'tp', xor_pairs(size, 2))  9.18 us
    ppermute x1, waiting for transfers between devices, local(): mine = mine + lax.ppermute(mine, 'tp', xor_pairs(size, 2))  9.18 us
    dot_general x2, matrix products, projected_blocks(): jnp.einsum('nrhc,hcd->nrd', attended, out_weight.reshape(attended.shape[2...  8.47 us
    dynamic_slice x4, local copies, waits for them, and re-layouts, attend_blocks(): lax.dynamic_slice_in_dim(keys_after_rotary, s, span)  6.94 us
    ppermute x1, waiting for transfers between devices, local(): lax.ppermute(message, 'tp', xor_pairs(size, 2)).astype(jnp.float32)  6.02 us
  transfers between devices with their start and end apart: 9, of which 7 were waited for; matrix products, arithmetic and copies ran while one was open for 25% of the time, Pallas kernels for 0%

profile of v2, /device:TPU:1, one launch (start us, length us, event | category | flops | bytes accessed | tf_op | source)
XLA Modules:
  0.0 145.4 jit_solution(8089397182439986274)
XLA Ops:
  1.9 1.5 %fusion.137 = (s32[240]{0:T(256)}, s32[240]{0:T(256)S(1)}, s32[240]{0:T(256)S(1)}, s32[240]{0:T(256)}) fusion(s32[960]{0:T(1024)} %param.19, s32[]{:T(128)S(6)} %select_n.73, s32[]{:T(128)S(6)} %select_n.76, s32[]{:T(128)S(6)} %select_n.75, s32[]{:T(128)S(6)} %select_n.74), kind=kLoop, calls=%fused_computation.206 | loop fusion | bytes 7696 | tf_op jit(solution)/shard_map/dynamic_slice | solution.py:52
  7.9 1.9 %copy.31 = bf16[960,128]{0,1:T(8,128)(2,1)} copy(bf16[960,128]{1,0:T(8,128)(2,1)} %param.12) | data formatting | bytes 491520 | tf_op args[1]
  10.8 1.8 %fusion.80 = (bf16[960,1,64]{0,2,1:T(8,128)(2,1)S(1)}, bf16[960,1,64]{0,2,1:T(8,128)(2,1)S(1)}) fusion(f32[960,1,128]{0,2,1:T(8,128)S(1)} %bitcast_convert_fusion, f32[64]{0:T(128)} %multiply_power_fusion, f32[960]{0:T(1024)S(1)} %get-tuple-element.44), kind=kLoop, calls=%fused_computation.124 | loop fusion | flops 552960 | bytes 741376 | tf_op jit(solution)/shard_map/convert.13
  12.6 1.4 fusion.87
  14.0 1.7 %copy.33 = bf16[720,1,128]{2,0,1:T(8,128)(2,1)} copy(bf16[720,1,128]{0,2,1:T(8,128)(2,1)} %get-tuple-element.25) | data formatting | bytes 368640 | tf_op jit(solution)/shard_map/dynamic_slice | solution.py:54
  15.7 1.7 %copy.32 = bf16[720,1,128]{2,0,1:T(8,128)(2,1)} copy(bf16[720,1,128]{0,2,1:T(8,128)(2,1)} %get-tuple-element.24) | data formatting | bytes 368640 | tf_op jit(solution)/shard_map/dynamic_slice | solution.py:54
  21.0 2.6 %multiply_cosine_fusion.1 = (f32[480,64]{1,0:T(8,128)}, f32[480,64]{1,0:T(8,128)}, f32[480,64]{1,0:T(8,128)S(1)}, f32[480,64]{1,0:T(8,128)S(1)}) fusion(f32[480]{0:T(512)S(1)} %get-tuple-element.56, f32[64]{0:T(128)S(1)} %copy-done.25, f32[480]{0:T(512)S(1)} %get-tuple-element.55), kind=kLoop, calls=%fused_computation.116 | loop fusion | flops 61440 | bytes 495616 | tf_op jit(solution)/shard_map/cos | solution.py:23
  24.3 6.6 %fusion.139 = f32[2,1920]{1,0:T(2,128)} fusion(s32[2,1920]{1,0:T(2,128)} %le.35, s32[2,720]{1,0:T(2,128)} %pad_add_fusion.3, s32[2,720]{1,0:T(2,128)} %pad_add_fusion.2, s32[2,1920]{1,0:T(2,128)} %eq.66, bf16[1,720,128]{2,1,0:T(8,128)(2,1)} %bitcast.129, bf16[1,720,128]{2,1,0:T(8,128)(2,1)} %bitcast.131, bf16[2,1920,64]{2,1,0:T(8,128)(2,1)S(1)} %bitcast.124, ...), kind=kOutput, calls=%fused_computation.208 | convolution fusion | flops 729293504 | bytes 1409280 | tf_op jit(solution)/shard_map/sub | solution.py:76
  30.9 8.9 %fusion.39 = bf16[2,240,8,128]{3,2,1,0:T(8,128)(2,1)} fusion(f32[2,1920]{1,0:T(2,128)} %fusion.139, bf16[1,720,128]{2,1,0:T(8,128)(2,1)} %get-tuple-element.28, bf16[1,720,128]{2,1,0:T(8,128)(2,1)} %get-tuple-element.29, s32[2,1920]{1,0:T(2,128)} %le.35, s32[2,720]{1,0:T(2,128)} %pad_add_fusion.3, s32[2,720]{1,0:T(2,128)} %pad_add_fusion.2, ...), kind=kOutput, calls=%fused_computation.64 | convolution fusion | flops 1440526848 | bytes 2760960 | tf_op jit(solution)/shard_map/nqk,nkd->nqd/dot_general | solution.py:78
  39.7 4.2 %convolution_bitcast_fusion.1 = f32[2,240,2048]{2,1,0:T(8,128)S(1)} fusion(bf16[8,128,2048,1]{2,1,0,3:T(8,128)(2,1)} %bitcast.148, bf16[2,240,8,128]{3,2,1,0:T(8,128)(2,1)} %fusion.39), kind=kOutput, calls=%fused_computation.26 | convolution fusion | flops 2013265920 | bytes 9109504 | tf_op jit(solution)/shard_map/nrhc,hcd->nrd/dot_general | solution.py:115
  44.0 1.8 %copy-done.1 = f32[2,240,2048]{2,1,0:T(8,128)} copy-done((f32[2,240,2048]{2,1,0:T(8,128)}, f32[2,240,2048]{2,1,0:T(8,128)S(1)}, u32[]{:S(2)}) %copy-start.1) | copy-done | bytes 3932184
  46.0 3.3 %collective-permute-start = (bf16[240,2048]{1,0:T(8,128)(2,1)S(1)}, bf16[240,2048]{1,0:T(8,128)(2,1)S(1)}, u32[]{:S(2)}, u32[]{:S(2)}) collective-permute-start(bf16[240,2048]{1,0:T(8,128)(2,1)S(1)} %fusion.54), channel_id=1, source_target_pairs={{0,1},{1,0},{2,3},{3,2},{4,5},{5,4},{6,7},{7,6},{8,9},{9,8},{10,11... | collective-permute-start | bytes 2949128 | tf_op jit(solution)/shard_map/ppermute | solution.py:121
  50.1 1.7 %le.31 = s32[2,1920]{1,0:T(2,128)} reshape(s32[2,240,8]{2,1,0:T(8,128)} %broadcast_in_dim.30) | data formatting | bytes 30720 | tf_op jit(solution)/shard_map/le | solution.py:72
  54.9 1.7 %copy.36 = bf16[720,1,128]{2,0,1:T(8,128)(2,1)} copy(bf16[720,1,128]{0,2,1:T(8,128)(2,1)} %get-tuple-element.26) | data formatting | bytes 368640 | tf_op jit(solution)/shard_map/dynamic_slice | solution.py:54
  56.6 1.7 %copy.35 = bf16[720,1,128]{2,0,1:T(8,128)(2,1)} copy(bf16[720,1,128]{0,2,1:T(8,128)(2,1)} %get-tuple-element.23) | data formatting | bytes 368640 | tf_op jit(solution)/shard_map/dynamic_slice | solution.py:54
  60.3 1.9 %fusion.134 = (bf16[240,2048]{1,0:T(8,128)(2,1)S(1)}, f32[240,2048]{1,0:T(8,128)S(1)}) fusion(bf16[240,2048]{1,0:T(8,128)(2,1)S(1)} %collective-permute-done, f32[2,240,2048]{2,1,0:T(8,128)} %copy-done.1), kind=kLoop, calls=%fused_computation.204 | loop fusion | flops 1474560 | bytes 5898240 | tf_op jit(solution)/shard_map/convert_element_type | solution.py:123
  66.2 2.0 %subtract_convert_fusion = (bf16[480,8,64]{2,1,0:T(8,128)(2,1)}, bf16[480,8,64]{2,1,0:T(8,128)(2,1)}) fusion(f32[480,8,128]{2,1,0:T(8,128)S(1)} %bitcast.117, f32[480,64]{1,0:T(8,128)S(1)} %copy-done.11, f32[480,64]{1,0:T(8,128)S(1)} %copy-done.10), kind=kLoop, calls=%fused_computation.52 | loop fusion | flops 1966080 | bytes 3194880 | tf_op jit(solution)/shard_map/convert.10
  68.2 6.2 %fusion.140 = f32[2,1920]{1,0:T(2,128)S(1)} fusion(s32[2,1920]{1,0:T(2,128)S(1)} %copy-done.16, s32[2,720]{1,0:T(2,128)S(1)} %copy-done.21, s32[2,720]{1,0:T(2,128)S(1)} %copy-done.22, s32[2,1920]{1,0:T(2,128)S(1)} %eq.62, bf16[1,720,128]{2,1,0:T(8,128)(2,1)} %bitcast.133, bf16[1,720,128]{2,1,0:T(8,128)(2,1)} %bitcast.135, ...), kind=kOutput, calls=%fused_computation.209 | convolution fusion | flops 729293504 | bytes 1409280 | tf_op jit(solution)/shard_map/sub | solution.py:76
  74.5 9.1 %fusion.40 = bf16[2,240,8,128]{3,2,1,0:T(8,128)(2,1)} fusion(f32[2,1920]{1,0:T(2,128)S(1)} %fusion.140, bf16[1,720,128]{2,1,0:T(8,128)(2,1)S(1)} %copy-done.13, bf16[1,720,128]{2,1,0:T(8,128)(2,1)S(1)} %copy-done.12, s32[2,1920]{1,0:T(2,128)S(1)} %copy-done.16, s32[2,720]{1,0:T(2,128)S(1)} %copy-done.21, s32[2,720]{1,0:T(2,128)S(1)} %copy-done.22, ...), kind=kOutput, calls=%fused_computation.65 | convolution fusion | flops 1440526848 | bytes 2760960 | tf_op jit(solution)/shard_map/nqk,nkd->nqd/dot_general | solution.py:78
  83.6 4.2 %convolution_bitcast_fusion = f32[2,240,2048]{2,1,0:T(8,128)S(1)} fusion(bf16[8,128,2048,1]{2,1,0,3:T(8,128)(2,1)} %bitcast.149, bf16[2,240,8,128]{3,2,1,0:T(8,128)(2,1)} %fusion.40), kind=kOutput, calls=%fused_computation.25 | convolution fusion | flops 2013265920 | bytes 9109504 | tf_op jit(solution)/shard_map/nrhc,hcd->nrd/dot_general | solution.py:115
  87.8 1.8 %copy-done.3 = f32[2,240,2048]{2,1,0:T(8,128)} copy-done((f32[2,240,2048]{2,1,0:T(8,128)}, f32[2,240,2048]{2,1,0:T(8,128)S(1)}, u32[]{:S(2)}) %copy-start.3) | copy-done | bytes 3932184
  92.7 6.0 %collective-permute-done.2 = bf16[240,3072]{1,0:T(8,128)(2,1)S(1)} collective-permute-done((bf16[240,3072]{1,0:T(8,128)(2,1)}, bf16[240,3072]{1,0:T(8,128)(2,1)S(1)}, u32[]{:S(2)}, u32[]{:S(2)}) %collective-permute-start.2) | collective-permute-done | bytes 1474592 | tf_op jit(solution)/shard_map/ppermute | solution.py:129
  101.2 1.8 %fusion.21 = (f32[240]{0:T(256)S(1)}, bf16[240,2048]{1,0:T(8,128)(2,1)S(1)}) fusion(f32[240,1024]{1,0:T(8,128)S(1)} %slice.91, f32[240,3072]{1,0:T(8,128)S(1)} %convert_element_type.149, bf16[240,2048]{1,0:T(8,128)(2,1)} %collective-permute-done.1, f32[2,240,2048]{2,1,0:T(8,128)S(1)} %copy-done.4, bf16[240,2048]{1,0:T(8,128)(2,1)S(1)} %copy-done.7), kind=kLoop, calls=%fused_computation.36 | loop fusion | flops 4914960 | bytes 7865280 | tf_op jit(solution)/shard_map/reduce_sum | solution.py:34
  105.8 1.7 %collective-permute-done.3 = bf16[2,80,2048]{2,1,0:T(8,128)(2,1)S(1)} collective-permute-done((bf16[2,80,2048]{2,1,0:T(8,128)(2,1)S(1)}, bf16[2,80,2048]{2,1,0:T(8,128)(2,1)S(1)}, u32[]{:S(2)}, u32[]{:S(2)}) %collective-permute-start.3) | collective-permute-done | bytes 655392 | tf_op jit(solution)/shard_map/ppermute | solution.py:158
  108.9 9.2 %collective-permute-done.4 = bf16[80,2048]{1,0:T(8,128)(2,1)S(1)} collective-permute-done((bf16[80,2048]{1,0:T(8,128)(2,1)S(1)}, bf16[80,2048]{1,0:T(8,128)(2,1)S(1)}, u32[]{:S(2)}, u32[]{:S(2)}) %collective-permute-start.4) | collective-permute-done | bytes 327712 | tf_op jit(solution)/shard_map/ppermute | solution.py:160
  118.1 1.6 %collective-permute-start.5 = (bf16[80,2048]{1,0:T(8,128)(2,1)S(1)}, bf16[80,2048]{1,0:T(8,128)(2,1)S(1)}, u32[]{:S(2)}, u32[]{:S(2)}) collective-permute-start(bf16[80,2048]{1,0:T(8,128)(2,1)S(1)} %add.251), channel_id=1, source_target_pairs={{0,1},{1,0},{2,3},{3,2},{4,5},{5,4},{6,7},{7,6},{8,9},{9,8},{10,11... | collective-permute-start | bytes 983048 | tf_op jit(solution)/shard_map/ppermute | solution.py:161
  121.7 2.0 %fusion.31 = f32[2,80,192]{2,1,0:T(8,128)S(1)} fusion(bf16[2,2,2048,192]{2,3,1,0:T(8,128)(2,1)} %param.17, bf16[1,80,2048]{2,1,0:T(8,128)(2,1)S(1)} %bitcast.151, bf16[1,80,2048]{2,1,0:T(8,128)(2,1)S(1)} %bitcast.127, pred[]{:T(512)S(6)} %eq.76), kind=kOutput, calls=%fused_computation.57 | convolution fusion | flops 126812160 | bytes 2351105 | tf_op jit(solution)/shard_map/ekd,edf->ekf/dot_general | solution.py:163
  123.7 2.6 %convolution_multiply_fusion = f32[2,80,2048]{2,1,0:T(8,128)S(1)} fusion(bf16[2,192,2048]{2,1,0:T(8,128)(2,1)S(1)} %copy-done, bf16[2,2,2048,192]{2,3,1,0:T(8,128)(2,1)} %param.17, f32[2,80]{1,0:T(2,128)S(1)} %select_reduce_fusion, f32[2,80,192]{2,1,0:T(8,128)S(1)} %fusion.31, bf16[1,80,2048]{2,1,0:T(8,128)(2,1)} %bitcast.152, ...), kind=kOutput, calls=%fused_computation.34 | convolution fusion | flops 253153280 | bytes 5235329 | tf_op jit(solution)/shard_map/ekf,efd->ekd/dot_general | solution.py:166
  126.8 2.7 %collective-permute-done.6 = f32[2,80,2048]{2,1,0:T(8,128)S(1)} collective-permute-done((f32[2,80,2048]{2,1,0:T(8,128)S(1)}, f32[2,80,2048]{2,1,0:T(8,128)S(1)}, u32[]{:S(2)}, u32[]{:S(2)}) %collective-permute-start.6) | collective-permute-done | bytes 1310752 | tf_op jit(solution)/shard_map/ppermute | solution.py:168
  130.9 9.2 %collective-permute-done.7 = bf16[80,2048]{1,0:T(8,128)(2,1)S(1)} collective-permute-done((bf16[80,2048]{1,0:T(8,128)(2,1)S(1)}, bf16[80,2048]{1,0:T(8,128)(2,1)S(1)}, u32[]{:S(2)}, u32[]{:S(2)}) %collective-permute-start.7) | collective-permute-done | bytes 327712 | tf_op jit(solution)/shard_map/ppermute | solution.py:170
  141.5 1.7 %collective-permute-done.8 = f32[80,2048]{1,0:T(8,128)S(1)} collective-permute-done((f32[80,2048]{1,0:T(8,128)S(1)}, f32[80,2048]{1,0:T(8,128)S(1)}, u32[]{:S(2)}, u32[]{:S(2)}) %collective-permute-start.8) | collective-permute-done | bytes 655392 | tf_op jit(solution)/shard_map/ppermute | solution.py:173
  143.2 2.2 %fusion.20 = bf16[240,2048]{1,0:T(8,128)(2,1)} fusion(bf16[240,2048]{1,0:T(8,128)(2,1)S(1)} %copy-done.9, f32[1,80,2048]{2,1,0:T(8,128)S(1)} %bitcast.150, f32[1,80,2048]{2,1,0:T(8,128)S(1)} %bitcast.126, pred[]{:T(512)S(6)} %eq.76, pred[2,80,960]{2,1,0:T(8,128)(4,1)S(1)} %fusion.64, s32[]{:T(128)S(6)} %select_n.74), kind=kOutput, calls=%fused_computation.33 | convolution fusion | flops 946176000 | bytes 3317765 | tf_op jit(solution)/shard_map/ekt,ekd->td/dot_general | solution.py:175
  (126 shorter events, 36.3 us)
Async XLA Ops:
  0.0 123.7 %copy-start = (bf16[2,192,2048]{2,1,0:T(8,128)(2,1)S(1)}, bf16[2,192,2048]{2,1,0:T(8,128)(2,1)}, u32[]{:S(2)}) copy-start(bf16[2,192,2048]{2,1,0:T(8,128)(2,1)} %param.18) | copy-start | bytes 4718596
  7.9 9.6 %copy-start.5 = (bf16[960,1024]{1,0:T(8,128)(2,1)S(1)}, bf16[960,1024]{1,0:T(8,128)(2,1)}, u32[]{:S(2)}) copy-start(bf16[960,1024]{1,0:T(8,128)(2,1)} %param.11) | copy-start | bytes 5898244
  17.8 1.9 %copy-start.17 = (s32[1,720]{1,0:T(1,128)S(1)}, s32[1,720]{1,0:T(1,128)}, u32[]{:S(2)}) copy-start(s32[1,720]{1,0:T(1,128)} %get-tuple-element.57) | copy-start | bytes 8644
  17.8 1.9 %copy-start.18 = (s32[1,720]{1,0:T(1,128)S(1)}, s32[1,720]{1,0:T(1,128)}, u32[]{:S(2)}) copy-start(s32[1,720]{1,0:T(1,128)} %get-tuple-element.58) | copy-start | bytes 8644
  17.8 2.5 %copy-start.19 = (s32[1,720]{1,0:T(1,128)S(1)}, s32[1,720]{1,0:T(1,128)}, u32[]{:S(2)}) copy-start(s32[1,720]{1,0:T(1,128)} %stack.132) | copy-start | bytes 8644
  17.8 2.5 %copy-start.20 = (s32[1,720]{1,0:T(1,128)S(1)}, s32[1,720]{1,0:T(1,128)}, u32[]{:S(2)}) copy-start(s32[1,720]{1,0:T(1,128)} %stack.131) | copy-start | bytes 8644
  17.8 3.2 %copy-start.25 = (f32[64]{0:T(128)S(1)}, f32[64]{0:T(128)}, u32[]{:S(2)}) copy-start(f32[64]{0:T(128)} %multiply_power_fusion) | copy-start | bytes 772
  44.0 1.9 %copy-start.1 = (f32[2,240,2048]{2,1,0:T(8,128)}, f32[2,240,2048]{2,1,0:T(8,128)S(1)}, u32[]{:S(2)}) copy-start(f32[2,240,2048]{2,1,0:T(8,128)S(1)} %convolution_bitcast_fusion.1) | copy-start | bytes 11796484
  45.8 3.4 %copy-start.23 = (s32[240]{0:T(256)S(1)}, s32[240]{0:T(256)}, u32[]{:S(2)}) copy-start(s32[240]{0:T(256)} %get-tuple-element.35) | copy-start | bytes 2884
  45.8 3.4 %copy-start.24 = (s32[240]{0:T(256)S(1)}, s32[240]{0:T(256)}, u32[]{:S(2)}) copy-start(s32[240]{0:T(256)} %get-tuple-element.38) | copy-start | bytes 2884
  46.0 14.3 %collective-permute-start = (bf16[240,2048]{1,0:T(8,128)(2,1)S(1)}, bf16[240,2048]{1,0:T(8,128)(2,1)S(1)}, u32[]{:S(2)}, u32[]{:S(2)}) collective-permute-start(bf16[240,2048]{1,0:T(8,128)(2,1)S(1)} %fusion.54), channel_id=1, source_target_pairs={{0,1},{1,0},{2,3},{3,2},{4,5},{5,4},{6,7},{7,6},{8,9},{9,8},{10,11... | collective-permute-start | bytes 2949128 | tf_op jit(solution)/shard_map/ppermute | solution.py:121
  62.2 2.6 %copy-start.6 = (bf16[960,1024]{1,0:T(8,128)(2,1)S(1)}, bf16[960,1024]{1,0:T(8,128)(2,1)}, u32[]{:S(2)}) copy-start(bf16[960,1024]{1,0:T(8,128)(2,1)} %param.11) | copy-start | bytes 5898244
  63.6 35.2 %collective-permute-start.2 = (bf16[240,3072]{1,0:T(8,128)(2,1)}, bf16[240,3072]{1,0:T(8,128)(2,1)S(1)}, u32[]{:S(2)}, u32[]{:S(2)}) collective-permute-start(bf16[240,3072]{1,0:T(8,128)(2,1)} %pad_maximum_fusion), channel_id=1, source_target_pairs={{0,2},{1,3},{2,0},{3,1},{4,6},{5,7},{6,4},{7,5},{8,10},{9,11},{10,... | collective-permute-start | bytes 4423688 | tf_op jit(solution)/shard_map/ppermute | solution.py:129
  66.1 2.0 %copy-start.16 = (s32[2,1920]{1,0:T(2,128)S(1)}, s32[2,1920]{1,0:T(2,128)}, u32[]{:S(2)}) copy-start(s32[2,1920]{1,0:T(2,128)} %le.31) | copy-start | bytes 46084
  66.2 2.0 %copy-start.21 = (s32[2,720]{1,0:T(2,128)S(1)}, s32[2,720]{1,0:T(2,128)}, u32[]{:S(2)}) copy-start(s32[2,720]{1,0:T(2,128)} %pad_add_fusion.1) | copy-start | bytes 17284
  66.2 2.0 %copy-start.22 = (s32[2,720]{1,0:T(2,128)S(1)}, s32[2,720]{1,0:T(2,128)}, u32[]{:S(2)}) copy-start(s32[2,720]{1,0:T(2,128)} %pad_add_fusion) | copy-start | bytes 17284
  68.2 6.3 %copy-start.12 = (bf16[1,720,128]{2,1,0:T(8,128)(2,1)S(1)}, bf16[1,720,128]{2,1,0:T(8,128)(2,1)}, u32[]{:S(2)}) copy-start(bf16[1,720,128]{2,1,0:T(8,128)(2,1)} %get-tuple-element.27) | copy-start | bytes 552964
  68.2 6.3 %copy-start.13 = (bf16[1,720,128]{2,1,0:T(8,128)(2,1)S(1)}, bf16[1,720,128]{2,1,0:T(8,128)(2,1)}, u32[]{:S(2)}) copy-start(bf16[1,720,128]{2,1,0:T(8,128)(2,1)} %get-tuple-element.30) | copy-start | bytes 552964
  87.8 1.9 %copy-start.3 = (f32[2,240,2048]{2,1,0:T(8,128)}, f32[2,240,2048]{2,1,0:T(8,128)S(1)}, u32[]{:S(2)}) copy-start(f32[2,240,2048]{2,1,0:T(8,128)S(1)} %convolution_bitcast_fusion) | copy-start | bytes 11796484
  89.6 1.8 %copy-start.14 = (s32[960,8]{0,1:T(8,128)S(1)}, s32[960,8]{0,1:T(8,128)}, u32[]{:S(2)}) copy-start(s32[960,8]{0,1:T(8,128)} %param.20) | copy-start | bytes 92164
  90.7 8.5 %collective-permute-start.1 = (bf16[240,2048]{1,0:T(8,128)(2,1)}, bf16[240,2048]{1,0:T(8,128)(2,1)}, u32[]{:S(2)}, u32[]{:S(2)}) collective-permute-start(bf16[240,2048]{1,0:T(8,128)(2,1)} %fusion.55), channel_id=1, source_target_pairs={{0,1},{1,0},{2,3},{3,2},{4,5},{5,4},{6,7},{7,6},{8,9},{9,8},{10,11... | collective-permute-start | bytes 2949128 | tf_op jit(solution)/shard_map/ppermute | solution.py:132
  98.7 1.2 copy-start.7
  98.8 2.3 %copy-start.4 = (f32[2,240,2048]{2,1,0:T(8,128)S(1)}, f32[2,240,2048]{2,1,0:T(8,128)}, u32[]{:S(2)}) copy-start(f32[2,240,2048]{2,1,0:T(8,128)} %copy-done.3) | copy-start | bytes 11796484
  99.2 4.8 %copy-start.27 = (f32[2048]{0:T(1024)S(1)}, f32[2048]{0:T(1024)}, u32[]{:S(2)}) copy-start(f32[2048]{0:T(1024)} %param.16) | copy-start | bytes 24580
  103.0 16.7 %copy-start.15 = (f32[960,8]{0,1:T(8,128)S(1)}, f32[960,8]{0,1:T(8,128)}, u32[]{:S(2)}) copy-start(f32[960,8]{0,1:T(8,128)} %param.21) | copy-start | bytes 92164
  104.4 3.1 %collective-permute-start.3 = (bf16[2,80,2048]{2,1,0:T(8,128)(2,1)S(1)}, bf16[2,80,2048]{2,1,0:T(8,128)(2,1)S(1)}, u32[]{:S(2)}, u32[]{:S(2)}) collective-permute-start(bf16[2,80,2048]{2,1,0:T(8,128)(2,1)S(1)} %convolution_convert_fusion), channel_id=1, source_target_pairs={{0,1},{1,0},{2,3},{3,2},{4,5},{5,4},{6,7},{7,6},{8,9},{9,8},{10,11... | collective-permute-start | bytes 1966088 | tf_op jit(solution)/shard_map/ppermute | solution.py:158
  107.6 10.5 %collective-permute-start.4 = (bf16[80,2048]{1,0:T(8,128)(2,1)S(1)}, bf16[80,2048]{1,0:T(8,128)(2,1)S(1)}, u32[]{:S(2)}, u32[]{:S(2)}) collective-permute-start(bf16[80,2048]{1,0:T(8,128)(2,1)S(1)} %fusion.76), channel_id=1, source_target_pairs={{0,2},{1,3},{2,0},{3,1},{4,6},{5,7},{6,4},{7,5},{8,10},{9,11},{10,... | collective-permute-start | bytes 983048 | tf_op jit(solution)/shard_map/ppermute | solution.py:160
  118.1 2.8 %collective-permute-start.5 = (bf16[80,2048]{1,0:T(8,128)(2,1)S(1)}, bf16[80,2048]{1,0:T(8,128)(2,1)S(1)}, u32[]{:S(2)}, u32[]{:S(2)}) collective-permute-start(bf16[80,2048]{1,0:T(8,128)(2,1)S(1)} %add.251), channel_id=1, source_target_pairs={{0,1},{1,0},{2,3},{3,2},{4,5},{5,4},{6,7},{7,6},{8,9},{9,8},{10,11... | collective-permute-start | bytes 983048 | tf_op jit(solution)/shard_map/ppermute | solution.py:161
  126.4 16.8 %copy-start.9 = (bf16[240,2048]{1,0:T(8,128)(2,1)S(1)}, bf16[240,2048]{1,0:T(8,128)(2,1)}, u32[]{:S(2)}) copy-start(bf16[240,2048]{1,0:T(8,128)(2,1)} %copy-done.8) | copy-start | bytes 2949124
  126.4 3.1 %collective-permute-start.6 = (f32[2,80,2048]{2,1,0:T(8,128)S(1)}, f32[2,80,2048]{2,1,0:T(8,128)S(1)}, u32[]{:S(2)}, u32[]{:S(2)}) collective-permute-start(f32[2,80,2048]{2,1,0:T(8,128)S(1)} %convolution_multiply_fusion), channel_id=1, source_target_pairs={{0,1},{1,0},{2,3},{3,2},{4,5},{5,4},{6,7},{7,6},{8,9},{9,8},{10,11... | collective-permute-start | bytes 3932168 | tf_op jit(solution)/shard_map/ppermute | solution.py:168
  129.6 10.5 %collective-permute-start.7 = (bf16[80,2048]{1,0:T(8,128)(2,1)S(1)}, bf16[80,2048]{1,0:T(8,128)(2,1)S(1)}, u32[]{:S(2)}, u32[]{:S(2)}) collective-permute-start(bf16[80,2048]{1,0:T(8,128)(2,1)S(1)} %fusion.83), channel_id=1, source_target_pairs={{0,2},{1,3},{2,0},{3,1},{4,6},{5,7},{6,4},{7,5},{8,10},{9,11},{10,... | collective-permute-start | bytes 983048 | tf_op jit(solution)/shard_map/ppermute | solution.py:170
  140.1 3.0 %collective-permute-start.8 = (f32[80,2048]{1,0:T(8,128)S(1)}, f32[80,2048]{1,0:T(8,128)S(1)}, u32[]{:S(2)}, u32[]{:S(2)}) collective-permute-start(f32[80,2048]{1,0:T(8,128)S(1)} %convert_add_fusion.1), channel_id=1, source_target_pairs={{0,1},{1,0},{2,3},{3,2},{4,5},{5,4},{6,7},{7,6},{8,9},{9,8},{10,11... | collective-permute-start | bytes 1966088 | tf_op jit(solution)/shard_map/ppermute | solution.py:173
  (5 other events, 4.6 us)

commit v3 on v2

--- a/solution.py
+++ b/solution.py
@@ -155,8 +155,7 @@
         preferred_element_type=jnp.float32,
     ).astype(jnp.bfloat16)
     on_core = me % 2
-    picked = picked + lax.ppermute(picked, "tp", xor_pairs(size, 1))
-    mine = picked[on_core]
+    mine = picked[on_core] + lax.ppermute(picked[1 - on_core], "tp", xor_pairs(size, 1))
     mine = mine + lax.ppermute(mine, "tp", xor_pairs(size, 2))
     other = lax.ppermute(mine, "tp", xor_pairs(size, 1))
     picked = jnp.where(on_core == 0, jnp.stack([mine, other]), jnp.stack([other, mine]))
@@ -165,8 +164,7 @@
     active = (jax.nn.silu(gate) * upward).astype(jnp.bfloat16)
     outputs = jnp.einsum("ekf,efd->ekd", active, down_weight, preferred_element_type=jnp.float32)
     scaled = route_sel[:, :, None] * outputs
-    scaled = scaled + lax.ppermute(scaled, "tp", xor_pairs(size, 1))
-    mine = scaled[on_core]
+    mine = scaled[on_core] + lax.ppermute(scaled[1 - on_core], "tp", xor_pairs(size, 1))
     mine = mine + lax.ppermute(
         mine.astype(jnp.bfloat16), "tp", xor_pairs(size, 2)
     ).astype(jnp.float32)

time: 146 us -> 145 us (level)
    unnamed x61 -> x59, local copies, waits for them, and re-layouts: 11.2 us -> 11.2 us
  transfers between devices with their start and end apart: 9 -> 9, of which waited for: 7 -> 7; matrix products, arithmetic and copies ran while one was open for 25% -> 26% of each run, Pallas kernels for 0% -> 0%
where the time goes in v3:
time: 145 us
  matrix products  46.6 us (32%)
  local copies, waits for them, and re-layouts  31.9 us (22%)
  waiting for transfers between devices  30.1 us (21%)
  other arithmetic  23.1 us (16%)
  starting transfers between devices  12.5 us (9%)
    dot_general x2, matrix products, attend_blocks(): jnp.einsum('nqk,nkd->nqd', weights, value_one, preferred_element_type=jnp...  18 us
    sub x2, matrix products, attend_blocks(): weights = jnp.exp(scores - peak)  12.8 us
    unnamed x59, local copies, waits for them, and re-layouts  11.2 us
    ppermute x1, waiting for transfers between devices, local(): mine = mine + lax.ppermute(mine, 'tp', xor_pairs(size, 2))  9.19 us
    ppermute x1, waiting for transfers between devices, local(): lax.ppermute(mine.astype(jnp.bfloat16), 'tp', xor_pairs(size, 2))  9.19 us
    dot_general x2, matrix products, projected_blocks(): jnp.einsum('nrhc,hcd->nrd', attended, out_weight.reshape(attended.shape[2...  8.47 us
    dynamic_slice x4, local copies, waits for them, and re-layouts, attend_blocks(): lax.dynamic_slice_in_dim(keys_after_rotary, s, span)  6.93 us
    ppermute x1, waiting for transfers between devices, local(): lax.ppermute(message, 'tp', xor_pairs(size, 2)).astype(jnp.float32)  6.01 us
  transfers between devices with their start and end apart: 9, of which 7 were waited for; matrix products, arithmetic and copies ran while one was open for 26% of the time, Pallas kernels for 0%

profile of v3, /device:TPU:1, one launch (start us, length us, event | category | flops | bytes accessed | tf_op | source)
XLA Modules:
  0.0 144.7 jit_solution(11932992135674357581)
XLA Ops:
  1.9 1.5 %fusion.135 = (s32[240]{0:T(256)}, s32[240]{0:T(256)S(1)}, s32[240]{0:T(256)S(1)}, s32[240]{0:T(256)}) fusion(s32[960]{0:T(1024)} %param.19, s32[]{:T(128)S(6)} %select_n.77, s32[]{:T(128)S(6)} %select_n.80, s32[]{:T(128)S(6)} %select_n.79, s32[]{:T(128)S(6)} %select_n.78), kind=kLoop, calls=%fused_computation.206 | loop fusion | bytes 7696 | tf_op jit(solution)/shard_map/dynamic_slice | solution.py:52
  7.9 1.9 %copy.31 = bf16[960,128]{0,1:T(8,128)(2,1)} copy(bf16[960,128]{1,0:T(8,128)(2,1)} %param.12) | data formatting | bytes 491520 | tf_op args[1]
  10.8 1.8 %fusion.78 = (bf16[960,1,64]{0,2,1:T(8,128)(2,1)S(1)}, bf16[960,1,64]{0,2,1:T(8,128)(2,1)S(1)}) fusion(f32[960,1,128]{0,2,1:T(8,128)S(1)} %bitcast_convert_fusion, f32[64]{0:T(128)} %multiply_power_fusion, f32[960]{0:T(1024)S(1)} %get-tuple-element.44), kind=kLoop, calls=%fused_computation.124 | loop fusion | flops 552960 | bytes 741376 | tf_op jit(solution)/shard_map/convert.13
  12.6 1.4 fusion.85
  14.0 1.7 %copy.33 = bf16[720,1,128]{2,0,1:T(8,128)(2,1)} copy(bf16[720,1,128]{0,2,1:T(8,128)(2,1)} %get-tuple-element.25) | data formatting | bytes 368640 | tf_op jit(solution)/shard_map/dynamic_slice | solution.py:54
  15.7 1.7 %copy.32 = bf16[720,1,128]{2,0,1:T(8,128)(2,1)} copy(bf16[720,1,128]{0,2,1:T(8,128)(2,1)} %get-tuple-element.24) | data formatting | bytes 368640 | tf_op jit(solution)/shard_map/dynamic_slice | solution.py:54
  21.0 2.6 %multiply_cosine_fusion.1 = (f32[480,64]{1,0:T(8,128)}, f32[480,64]{1,0:T(8,128)}, f32[480,64]{1,0:T(8,128)S(1)}, f32[480,64]{1,0:T(8,128)S(1)}) fusion(f32[480]{0:T(512)S(1)} %get-tuple-element.56, f32[64]{0:T(128)S(1)} %copy-done.24, f32[480]{0:T(512)S(1)} %get-tuple-element.55), kind=kLoop, calls=%fused_computation.116 | loop fusion | flops 61440 | bytes 495616 | tf_op jit(solution)/shard_map/cos | solution.py:23
  24.3 6.6 %fusion.137 = f32[2,1920]{1,0:T(2,128)} fusion(s32[2,1920]{1,0:T(2,128)} %le.35, s32[2,720]{1,0:T(2,128)} %pad_add_fusion.3, s32[2,720]{1,0:T(2,128)} %pad_add_fusion.2, s32[2,1920]{1,0:T(2,128)} %eq.66, bf16[1,720,128]{2,1,0:T(8,128)(2,1)} %bitcast.133, bf16[1,720,128]{2,1,0:T(8,128)(2,1)} %bitcast.135, bf16[2,1920,64]{2,1,0:T(8,128)(2,1)S(1)} %bitcast.128, ...), kind=kOutput, calls=%fused_computation.208 | convolution fusion | flops 729293504 | bytes 1409280 | tf_op jit(solution)/shard_map/sub | solution.py:76
  30.8 8.9 %fusion.39 = bf16[2,240,8,128]{3,2,1,0:T(8,128)(2,1)} fusion(f32[2,1920]{1,0:T(2,128)} %fusion.137, bf16[1,720,128]{2,1,0:T(8,128)(2,1)} %get-tuple-element.28, bf16[1,720,128]{2,1,0:T(8,128)(2,1)} %get-tuple-element.29, s32[2,1920]{1,0:T(2,128)} %le.35, s32[2,720]{1,0:T(2,128)} %pad_add_fusion.3, s32[2,720]{1,0:T(2,128)} %pad_add_fusion.2, ...), kind=kOutput, calls=%fused_computation.64 | convolution fusion | flops 1440526848 | bytes 2760960 | tf_op jit(solution)/shard_map/nqk,nkd->nqd/dot_general | solution.py:78
  39.7 4.2 %convolution_bitcast_fusion.1 = f32[2,240,2048]{2,1,0:T(8,128)S(1)} fusion(bf16[8,128,2048,1]{2,1,0,3:T(8,128)(2,1)} %bitcast.152, bf16[2,240,8,128]{3,2,1,0:T(8,128)(2,1)} %fusion.39), kind=kOutput, calls=%fused_computation.26 | convolution fusion | flops 2013265920 | bytes 9109504 | tf_op jit(solution)/shard_map/nrhc,hcd->nrd/dot_general | solution.py:115
  44.0 1.8 %copy-done.1 = f32[2,240,2048]{2,1,0:T(8,128)} copy-done((f32[2,240,2048]{2,1,0:T(8,128)}, f32[2,240,2048]{2,1,0:T(8,128)S(1)}, u32[]{:S(2)}) %copy-start.1) | copy-done | bytes 3932184
  46.0 3.3 %collective-permute-start = (bf16[240,2048]{1,0:T(8,128)(2,1)S(1)}, bf16[240,2048]{1,0:T(8,128)(2,1)S(1)}, u32[]{:S(2)}, u32[]{:S(2)}) collective-permute-start(bf16[240,2048]{1,0:T(8,128)(2,1)S(1)} %fusion.54), channel_id=1, source_target_pairs={{0,1},{1,0},{2,3},{3,2},{4,5},{5,4},{6,7},{7,6},{8,9},{9,8},{10,11... | collective-permute-start | bytes 2949128 | tf_op jit(solution)/shard_map/ppermute | solution.py:121
  50.8 1.7 %le.31 = s32[2,1920]{1,0:T(2,128)} reshape(s32[2,240,8]{2,1,0:T(8,128)} %broadcast_in_dim.30) | data formatting | bytes 30720 | tf_op jit(solution)/shard_map/le | solution.py:72
  55.6 1.7 %copy.36 = bf16[720,1,128]{2,0,1:T(8,128)(2,1)} copy(bf16[720,1,128]{0,2,1:T(8,128)(2,1)} %get-tuple-element.26) | data formatting | bytes 368640 | tf_op jit(solution)/shard_map/dynamic_slice | solution.py:54
  57.3 1.7 %copy.35 = bf16[720,1,128]{2,0,1:T(8,128)(2,1)} copy(bf16[720,1,128]{0,2,1:T(8,128)(2,1)} %get-tuple-element.23) | data formatting | bytes 368640 | tf_op jit(solution)/shard_map/dynamic_slice | solution.py:54
  60.9 1.9 %fusion.132 = (bf16[240,2048]{1,0:T(8,128)(2,1)S(1)}, f32[240,2048]{1,0:T(8,128)S(1)}) fusion(bf16[240,2048]{1,0:T(8,128)(2,1)S(1)} %collective-permute-done, f32[2,240,2048]{2,1,0:T(8,128)} %copy-done.1), kind=kLoop, calls=%fused_computation.204 | loop fusion | flops 1474560 | bytes 5898240 | tf_op jit(solution)/shard_map/convert_element_type | solution.py:123
  66.8 2.0 %subtract_convert_fusion = (bf16[480,8,64]{2,1,0:T(8,128)(2,1)}, bf16[480,8,64]{2,1,0:T(8,128)(2,1)}) fusion(f32[480,8,128]{2,1,0:T(8,128)S(1)} %bitcast.121, f32[480,64]{1,0:T(8,128)S(1)} %copy-done.11, f32[480,64]{1,0:T(8,128)S(1)} %copy-done.10), kind=kLoop, calls=%fused_computation.52 | loop fusion | flops 1966080 | bytes 3194880 | tf_op jit(solution)/shard_map/convert.10
  68.8 6.2 %fusion.138 = f32[2,1920]{1,0:T(2,128)S(1)} fusion(s32[2,1920]{1,0:T(2,128)S(1)} %copy-done.16, s32[2,720]{1,0:T(2,128)S(1)} %copy-done.21, s32[2,720]{1,0:T(2,128)S(1)} %copy-done.22, s32[2,1920]{1,0:T(2,128)S(1)} %eq.62, bf16[1,720,128]{2,1,0:T(8,128)(2,1)} %bitcast.137, bf16[1,720,128]{2,1,0:T(8,128)(2,1)} %bitcast.139, ...), kind=kOutput, calls=%fused_computation.209 | convolution fusion | flops 729293504 | bytes 1409280 | tf_op jit(solution)/shard_map/sub | solution.py:76
  75.1 9.1 %fusion.40 = bf16[2,240,8,128]{3,2,1,0:T(8,128)(2,1)} fusion(f32[2,1920]{1,0:T(2,128)S(1)} %fusion.138, bf16[1,720,128]{2,1,0:T(8,128)(2,1)S(1)} %copy-done.13, bf16[1,720,128]{2,1,0:T(8,128)(2,1)S(1)} %copy-done.12, s32[2,1920]{1,0:T(2,128)S(1)} %copy-done.16, s32[2,720]{1,0:T(2,128)S(1)} %copy-done.21, s32[2,720]{1,0:T(2,128)S(1)} %copy-done.22, ...), kind=kOutput, calls=%fused_computation.65 | convolution fusion | flops 1440526848 | bytes 2760960 | tf_op jit(solution)/shard_map/nqk,nkd->nqd/dot_general | solution.py:78
  84.1 4.2 %convolution_bitcast_fusion = f32[2,240,2048]{2,1,0:T(8,128)S(1)} fusion(bf16[8,128,2048,1]{2,1,0,3:T(8,128)(2,1)} %bitcast.153, bf16[2,240,8,128]{3,2,1,0:T(8,128)(2,1)} %fusion.40), kind=kOutput, calls=%fused_computation.25 | convolution fusion | flops 2013265920 | bytes 9109504 | tf_op jit(solution)/shard_map/nrhc,hcd->nrd/dot_general | solution.py:115
  88.4 1.8 %copy-done.3 = f32[2,240,2048]{2,1,0:T(8,128)} copy-done((f32[2,240,2048]{2,1,0:T(8,128)}, f32[2,240,2048]{2,1,0:T(8,128)S(1)}, u32[]{:S(2)}) %copy-start.3) | copy-done | bytes 3932184
  93.3 6.0 %collective-permute-done.2 = bf16[240,3072]{1,0:T(8,128)(2,1)S(1)} collective-permute-done((bf16[240,3072]{1,0:T(8,128)(2,1)}, bf16[240,3072]{1,0:T(8,128)(2,1)S(1)}, u32[]{:S(2)}, u32[]{:S(2)}) %collective-permute-start.2) | collective-permute-done | bytes 1474592 | tf_op jit(solution)/shard_map/ppermute | solution.py:129
  101.8 1.8 %fusion.21 = (f32[240]{0:T(256)S(1)}, bf16[240,2048]{1,0:T(8,128)(2,1)S(1)}) fusion(f32[240,1024]{1,0:T(8,128)S(1)} %slice.91, f32[240,3072]{1,0:T(8,128)S(1)} %convert_element_type.149, bf16[240,2048]{1,0:T(8,128)(2,1)} %collective-permute-done.1, f32[2,240,2048]{2,1,0:T(8,128)S(1)} %copy-done.4, bf16[240,2048]{1,0:T(8,128)(2,1)S(1)} %copy-done.7), kind=kLoop, calls=%fused_computation.36 | loop fusion | flops 4914960 | bytes 7865280 | tf_op jit(solution)/shard_map/reduce_sum | solution.py:34
  105.1 1.4 collective-permute-start.3
  109.1 9.2 %collective-permute-done.4 = bf16[80,2048]{1,0:T(8,128)(2,1)S(1)} collective-permute-done((bf16[80,2048]{1,0:T(8,128)(2,1)S(1)}, bf16[80,2048]{1,0:T(8,128)(2,1)S(1)}, u32[]{:S(2)}, u32[]{:S(2)}) %collective-permute-start.4) | collective-permute-done | bytes 327712 | tf_op jit(solution)/shard_map/ppermute | solution.py:159
  118.3 1.6 %collective-permute-start.5 = (bf16[80,2048]{1,0:T(8,128)(2,1)S(1)}, bf16[80,2048]{1,0:T(8,128)(2,1)S(1)}, u32[]{:S(2)}, u32[]{:S(2)}) collective-permute-start(bf16[80,2048]{1,0:T(8,128)(2,1)S(1)} %add.257), channel_id=1, source_target_pairs={{0,1},{1,0},{2,3},{3,2},{4,5},{5,4},{6,7},{7,6},{8,9},{9,8},{10,11... | collective-permute-start | bytes 983048 | tf_op jit(solution)/shard_map/ppermute | solution.py:160
  121.9 2.0 %fusion.31 = f32[2,80,192]{2,1,0:T(8,128)S(1)} fusion(bf16[2,2,2048,192]{2,3,1,0:T(8,128)(2,1)} %param.17, bf16[1,80,2048]{2,1,0:T(8,128)(2,1)S(1)} %bitcast.155, bf16[1,80,2048]{2,1,0:T(8,128)(2,1)S(1)} %bitcast.131, pred[]{:T(512)S(6)} %eq.76), kind=kOutput, calls=%fused_computation.57 | convolution fusion | flops 126812160 | bytes 2351105 | tf_op jit(solution)/shard_map/ekd,edf->ekf/dot_general | solution.py:162
  123.9 2.6 %convolution_multiply_fusion = f32[2,80,2048]{2,1,0:T(8,128)S(1)} fusion(bf16[2,192,2048]{2,1,0:T(8,128)(2,1)S(1)} %copy-done, bf16[2,2,2048,192]{2,3,1,0:T(8,128)(2,1)} %param.17, f32[2,80]{1,0:T(2,128)S(1)} %select_reduce_fusion, f32[2,80,192]{2,1,0:T(8,128)S(1)} %fusion.31, bf16[1,80,2048]{2,1,0:T(8,128)(2,1)} %bitcast.156, ...), kind=kOutput, calls=%fused_computation.34 | convolution fusion | flops 253153280 | bytes 5235329 | tf_op jit(solution)/shard_map/ekf,efd->ekd/dot_general | solution.py:165
  127.1 1.7 %collective-permute-done.6 = f32[80,2048]{1,0:T(8,128)S(1)} collective-permute-done((f32[80,2048]{1,0:T(8,128)S(1)}, f32[80,2048]{1,0:T(8,128)S(1)}, u32[]{:S(2)}, u32[]{:S(2)}) %collective-permute-start.6) | collective-permute-done | bytes 655392 | tf_op jit(solution)/shard_map/ppermute | solution.py:167
  130.2 9.2 %collective-permute-done.7 = bf16[80,2048]{1,0:T(8,128)(2,1)S(1)} collective-permute-done((bf16[80,2048]{1,0:T(8,128)(2,1)S(1)}, bf16[80,2048]{1,0:T(8,128)(2,1)S(1)}, u32[]{:S(2)}, u32[]{:S(2)}) %collective-permute-start.7) | collective-permute-done | bytes 327712 | tf_op jit(solution)/shard_map/ppermute | solution.py:168
  140.8 1.7 %collective-permute-done.8 = f32[80,2048]{1,0:T(8,128)S(1)} collective-permute-done((f32[80,2048]{1,0:T(8,128)S(1)}, f32[80,2048]{1,0:T(8,128)S(1)}, u32[]{:S(2)}, u32[]{:S(2)}) %collective-permute-start.8) | collective-permute-done | bytes 655392 | tf_op jit(solution)/shard_map/ppermute | solution.py:171
  142.5 2.2 %fusion.20 = bf16[240,2048]{1,0:T(8,128)(2,1)} fusion(bf16[240,2048]{1,0:T(8,128)(2,1)S(1)} %copy-done.9, f32[1,80,2048]{2,1,0:T(8,128)S(1)} %bitcast.154, f32[1,80,2048]{2,1,0:T(8,128)S(1)} %bitcast.130, pred[]{:T(512)S(6)} %eq.76, pred[2,80,960]{2,1,0:T(8,128)(4,1)S(1)} %fusion.63, s32[]{:T(128)S(6)} %select_n.78), kind=kOutput, calls=%fused_computation.33 | convolution fusion | flops 946176000 | bytes 3317765 | tf_op jit(solution)/shard_map/ekt,ekd->td/dot_general | solution.py:173
  (126 shorter events, 36.9 us)
Async XLA Ops:
  0.0 123.9 %copy-start = (bf16[2,192,2048]{2,1,0:T(8,128)(2,1)S(1)}, bf16[2,192,2048]{2,1,0:T(8,128)(2,1)}, u32[]{:S(2)}) copy-start(bf16[2,192,2048]{2,1,0:T(8,128)(2,1)} %param.18) | copy-start | bytes 4718596
  7.9 9.6 %copy-start.5 = (bf16[960,1024]{1,0:T(8,128)(2,1)S(1)}, bf16[960,1024]{1,0:T(8,128)(2,1)}, u32[]{:S(2)}) copy-start(bf16[960,1024]{1,0:T(8,128)(2,1)} %param.11) | copy-start | bytes 5898244
  17.8 1.9 %copy-start.17 = (s32[1,720]{1,0:T(1,128)S(1)}, s32[1,720]{1,0:T(1,128)}, u32[]{:S(2)}) copy-start(s32[1,720]{1,0:T(1,128)} %get-tuple-element.57) | copy-start | bytes 8644
  17.8 1.9 %copy-start.18 = (s32[1,720]{1,0:T(1,128)S(1)}, s32[1,720]{1,0:T(1,128)}, u32[]{:S(2)}) copy-start(s32[1,720]{1,0:T(1,128)} %get-tuple-element.58) | copy-start | bytes 8644
  17.8 2.5 %copy-start.19 = (s32[1,720]{1,0:T(1,128)S(1)}, s32[1,720]{1,0:T(1,128)}, u32[]{:S(2)}) copy-start(s32[1,720]{1,0:T(1,128)} %stack.132) | copy-start | bytes 8644
  17.8 2.5 %copy-start.20 = (s32[1,720]{1,0:T(1,128)S(1)}, s32[1,720]{1,0:T(1,128)}, u32[]{:S(2)}) copy-start(s32[1,720]{1,0:T(1,128)} %stack.131) | copy-start | bytes 8644
  17.8 3.2 %copy-start.24 = (f32[64]{0:T(128)S(1)}, f32[64]{0:T(128)}, u32[]{:S(2)}) copy-start(f32[64]{0:T(128)} %multiply_power_fusion) | copy-start | bytes 772
  44.0 1.9 %copy-start.1 = (f32[2,240,2048]{2,1,0:T(8,128)}, f32[2,240,2048]{2,1,0:T(8,128)S(1)}, u32[]{:S(2)}) copy-start(f32[2,240,2048]{2,1,0:T(8,128)S(1)} %convolution_bitcast_fusion.1) | copy-start | bytes 11796484
  45.8 3.4 %copy-start.23 = (s32[240]{0:T(256)S(1)}, s32[240]{0:T(256)}, u32[]{:S(2)}) copy-start(s32[240]{0:T(256)} %get-tuple-element.35) | copy-start | bytes 2884
  46.0 15.0 %collective-permute-start = (bf16[240,2048]{1,0:T(8,128)(2,1)S(1)}, bf16[240,2048]{1,0:T(8,128)(2,1)S(1)}, u32[]{:S(2)}, u32[]{:S(2)}) collective-permute-start(bf16[240,2048]{1,0:T(8,128)(2,1)S(1)} %fusion.54), channel_id=1, source_target_pairs={{0,1},{1,0},{2,3},{3,2},{4,5},{5,4},{6,7},{7,6},{8,9},{9,8},{10,11... | collective-permute-start | bytes 2949128 | tf_op jit(solution)/shard_map/ppermute | solution.py:121
  62.8 2.6 %copy-start.6 = (bf16[960,1024]{1,0:T(8,128)(2,1)S(1)}, bf16[960,1024]{1,0:T(8,128)(2,1)}, u32[]{:S(2)}) copy-start(bf16[960,1024]{1,0:T(8,128)(2,1)} %param.11) | copy-start | bytes 5898244
  64.2 35.1 %collective-permute-start.2 = (bf16[240,3072]{1,0:T(8,128)(2,1)}, bf16[240,3072]{1,0:T(8,128)(2,1)S(1)}, u32[]{:S(2)}, u32[]{:S(2)}) collective-permute-start(bf16[240,3072]{1,0:T(8,128)(2,1)} %pad_maximum_fusion), channel_id=1, source_target_pairs={{0,2},{1,3},{2,0},{3,1},{4,6},{5,7},{6,4},{7,5},{8,10},{9,11},{10,... | collective-permute-start | bytes 4423688 | tf_op jit(solution)/shard_map/ppermute | solution.py:129
  65.7 1.1 copy-start.11
  66.8 2.0 %copy-start.16 = (s32[2,1920]{1,0:T(2,128)S(1)}, s32[2,1920]{1,0:T(2,128)}, u32[]{:S(2)}) copy-start(s32[2,1920]{1,0:T(2,128)} %le.31) | copy-start | bytes 46084
  66.8 2.0 %copy-start.21 = (s32[2,720]{1,0:T(2,128)S(1)}, s32[2,720]{1,0:T(2,128)}, u32[]{:S(2)}) copy-start(s32[2,720]{1,0:T(2,128)} %pad_add_fusion.1) | copy-start | bytes 17284
  66.8 2.0 %copy-start.22 = (s32[2,720]{1,0:T(2,128)S(1)}, s32[2,720]{1,0:T(2,128)}, u32[]{:S(2)}) copy-start(s32[2,720]{1,0:T(2,128)} %pad_add_fusion) | copy-start | bytes 17284
  68.8 6.3 %copy-start.12 = (bf16[1,720,128]{2,1,0:T(8,128)(2,1)S(1)}, bf16[1,720,128]{2,1,0:T(8,128)(2,1)}, u32[]{:S(2)}) copy-start(bf16[1,720,128]{2,1,0:T(8,128)(2,1)} %get-tuple-element.27) | copy-start | bytes 552964
  68.8 6.3 %copy-start.13 = (bf16[1,720,128]{2,1,0:T(8,128)(2,1)S(1)}, bf16[1,720,128]{2,1,0:T(8,128)(2,1)}, u32[]{:S(2)}) copy-start(bf16[1,720,128]{2,1,0:T(8,128)(2,1)} %get-tuple-element.30) | copy-start | bytes 552964
  88.4 1.9 %copy-start.3 = (f32[2,240,2048]{2,1,0:T(8,128)}, f32[2,240,2048]{2,1,0:T(8,128)S(1)}, u32[]{:S(2)}) copy-start(f32[2,240,2048]{2,1,0:T(8,128)S(1)} %convolution_bitcast_fusion) | copy-start | bytes 11796484
  90.2 1.8 %copy-start.14 = (s32[960,8]{0,1:T(8,128)S(1)}, s32[960,8]{0,1:T(8,128)}, u32[]{:S(2)}) copy-start(s32[960,8]{0,1:T(8,128)} %param.20) | copy-start | bytes 92164
  91.3 8.5 %collective-permute-start.1 = (bf16[240,2048]{1,0:T(8,128)(2,1)}, bf16[240,2048]{1,0:T(8,128)(2,1)}, u32[]{:S(2)}, u32[]{:S(2)}) collective-permute-start(bf16[240,2048]{1,0:T(8,128)(2,1)} %fusion.55), channel_id=1, source_target_pairs={{0,1},{1,0},{2,3},{3,2},{4,5},{5,4},{6,7},{7,6},{8,9},{9,8},{10,11... | collective-permute-start | bytes 2949128 | tf_op jit(solution)/shard_map/ppermute | solution.py:132
  99.3 1.2 copy-start.7
  99.4 2.3 %copy-start.4 = (f32[2,240,2048]{2,1,0:T(8,128)S(1)}, f32[2,240,2048]{2,1,0:T(8,128)}, u32[]{:S(2)}) copy-start(f32[2,240,2048]{2,1,0:T(8,128)} %copy-done.3) | copy-start | bytes 11796484
  99.8 4.8 %copy-start.26 = (f32[2048]{0:T(1024)S(1)}, f32[2048]{0:T(1024)}, u32[]{:S(2)}) copy-start(f32[2048]{0:T(1024)} %param.16) | copy-start | bytes 24580
  104.6 15.3 %copy-start.15 = (f32[960,8]{0,1:T(8,128)S(1)}, f32[960,8]{0,1:T(8,128)}, u32[]{:S(2)}) copy-start(f32[960,8]{0,1:T(8,128)} %param.21) | copy-start | bytes 92164
  105.1 2.6 %collective-permute-start.3 = (bf16[80,2048]{1,0:T(8,128)(2,1)S(1)}, bf16[80,2048]{1,0:T(8,128)(2,1)S(1)}, u32[]{:S(2)}, u32[]{:S(2)}) collective-permute-start(bf16[80,2048]{1,0:T(8,128)(2,1)S(1)} %dynamic-slice_bitcast_fusion.1), channel_id=1, source_target_pairs={{0,1},{1,0},{2,3},{3,2},{4,5},{5,4},{6,7},{7,6},{8,9},{9,8},{10,11... | collective-permute-start | bytes 983048 | tf_op jit(solution)/shard_map/ppermute | solution.py:158
  107.7 10.5 %collective-permute-start.4 = (bf16[80,2048]{1,0:T(8,128)(2,1)S(1)}, bf16[80,2048]{1,0:T(8,128)(2,1)S(1)}, u32[]{:S(2)}, u32[]{:S(2)}) collective-permute-start(bf16[80,2048]{1,0:T(8,128)(2,1)S(1)} %bitcast_add_fusion.1), channel_id=1, source_target_pairs={{0,2},{1,3},{2,0},{3,1},{4,6},{5,7},{6,4},{7,5},{8,10},{9,11},{10,... | collective-permute-start | bytes 983048 | tf_op jit(solution)/shard_map/ppermute | solution.py:159
  118.3 2.8 %collective-permute-start.5 = (bf16[80,2048]{1,0:T(8,128)(2,1)S(1)}, bf16[80,2048]{1,0:T(8,128)(2,1)S(1)}, u32[]{:S(2)}, u32[]{:S(2)}) collective-permute-start(bf16[80,2048]{1,0:T(8,128)(2,1)S(1)} %add.257), channel_id=1, source_target_pairs={{0,1},{1,0},{2,3},{3,2},{4,5},{5,4},{6,7},{7,6},{8,9},{9,8},{10,11... | collective-permute-start | bytes 983048 | tf_op jit(solution)/shard_map/ppermute | solution.py:160
  126.6 15.9 %copy-start.9 = (bf16[240,2048]{1,0:T(8,128)(2,1)S(1)}, bf16[240,2048]{1,0:T(8,128)(2,1)}, u32[]{:S(2)}) copy-start(bf16[240,2048]{1,0:T(8,128)(2,1)} %copy-done.8) | copy-start | bytes 2949124
  126.6 2.2 %collective-permute-start.6 = (f32[80,2048]{1,0:T(8,128)S(1)}, f32[80,2048]{1,0:T(8,128)S(1)}, u32[]{:S(2)}, u32[]{:S(2)}) collective-permute-start(f32[80,2048]{1,0:T(8,128)S(1)} %dynamic-slice_bitcast_fusion), channel_id=1, source_target_pairs={{0,1},{1,0},{2,3},{3,2},{4,5},{5,4},{6,7},{7,6},{8,9},{9,8},{10,11... | collective-permute-start | bytes 1966088 | tf_op jit(solution)/shard_map/ppermute | solution.py:167
  128.9 10.5 %collective-permute-start.7 = (bf16[80,2048]{1,0:T(8,128)(2,1)S(1)}, bf16[80,2048]{1,0:T(8,128)(2,1)S(1)}, u32[]{:S(2)}, u32[]{:S(2)}) collective-permute-start(bf16[80,2048]{1,0:T(8,128)(2,1)S(1)} %fusion.79), channel_id=1, source_target_pairs={{0,2},{1,3},{2,0},{3,1},{4,6},{5,7},{6,4},{7,5},{8,10},{9,11},{10,... | collective-permute-start | bytes 983048 | tf_op jit(solution)/shard_map/ppermute | solution.py:168
  139.5 3.0 %collective-permute-start.8 = (f32[80,2048]{1,0:T(8,128)S(1)}, f32[80,2048]{1,0:T(8,128)S(1)}, u32[]{:S(2)}, u32[]{:S(2)}) collective-permute-start(f32[80,2048]{1,0:T(8,128)S(1)} %convert_add_fusion.1), channel_id=1, source_target_pairs={{0,1},{1,0},{2,3},{3,2},{4,5},{5,4},{6,7},{7,6},{8,9},{9,8},{10,11... | collective-permute-start | bytes 1966088 | tf_op jit(solution)/shard_map/ppermute | solution.py:171
  (4 other events, 3.6 us)
